TPU v7x, 32 devices: a whole 2x2x4 slice. The times are simulated.
32 devices in a mesh: ctx: 8 (over y, x, core), tp: 4 (over z).
Axes of the slice: x: 2, y: 2, z: 4, core: 2. Of those that a mesh axis runs over, the one named last changes fastest.
Arguments:
- tokens: bfloat16 [4096, 4096], P(('ctx', 'tp')), may hold values from -6 to 6
- spike_query: int32 [4096, 32], P('ctx', 'tp'), may hold values 0 or 1
- spike_key: int32 [4096, 32], P('ctx', 'tp'), may hold values 0 or 1
- qkv_weight: bfloat16 [4096, 3, 4096], P(None, None, 'tp'), may hold values from -0.09375 to 0.09375
- qkv_blocks: int32 [3, 32, 32], P(None, None, 'tp'), may hold values 0 or 1
- out_weight: bfloat16 [4096, 4096], P('tp'), may hold values from -0.09375 to 0.09375
- out_blocks: int32 [32, 32], P('tp'), may hold values 0 or 1
- cotangent: bfloat16 [4096, 4096], P(('ctx', 'tp')), may hold values from -6 to 6
Outputs:
- layer_out: bfloat16 [4096, 4096], P(('ctx', 'tp'))
- token_grad: bfloat16 [4096, 4096], P(('ctx', 'tp'))
- qkv_grad: float32 [4096, 3, 4096], P('ctx', None, 'tp')
- out_grad: float32 [4096, 4096], P('tp', 'ctx')
All inputs are finite; a program needn't handle non-finite values. No bound on the sum of `spike_query` or of `spike_key` or of `qkv_blocks` or of `out_blocks` on one device may be relied on, other than what follows from the above.
Results may differ from a plain program's by a relative error of at most 0.014.
Values may be sent and summed in bfloat16 or wider, within the bound.
No kernel may reach another device: no remote copies, remote signals or barrier semaphores. Data moves between devices by JAX's collectives and lax.ppermute only.
A program may use at most 320 MiB of HBM per device.

v0:
```python
import math

import jax
import jax.numpy as jnp
from jax import lax
from jax.experimental import pallas as pl
from jax.experimental.pallas import tpu as pltpu
from jax.sharding import PartitionSpec as P

BLOCK = 128


EPSILON = 1e-05

def _tile(n, choices=(1024, 512, 256, 128)):
    for c in choices:
        if n % c == 0:
            return c
    return n


def _masked_tile(w_ref, m_ref, wm_ref):
    for g in range(w_ref.shape[0] // BLOCK):
        rows = slice(g * BLOCK, (g + 1) * BLOCK)
        wm_ref[rows, :] = w_ref[rows, :] * m_ref[g]


def _nn_kernel(a_ref, w_ref, m_ref, o_ref, acc_ref, wm_ref):
    k = pl.program_id(2)

    @pl.when(k == 0)
    def _():
        acc_ref[...] = jnp.zeros_like(acc_ref)

    _masked_tile(w_ref, m_ref, wm_ref)
    acc_ref[...] += jnp.dot(a_ref[...], wm_ref[...], preferred_element_type=jnp.float32)

    @pl.when(k == pl.num_programs(2) - 1)
    def _():
        o_ref[...] = acc_ref[...].astype(o_ref.dtype)


def _nt_kernel(a_ref, w_ref, m_ref, o_ref, acc_ref, wm_ref):
    p = pl.program_id(1)
    k = pl.program_id(2)

    @pl.when((p == 0) & (k == 0))
    def _():
        acc_ref[...] = jnp.zeros_like(acc_ref)

    _masked_tile(w_ref, m_ref, wm_ref)
    acc_ref[...] += lax.dot_general(
        a_ref[...], wm_ref[...], (((1,), (1,)), ((), ())), preferred_element_type=jnp.float32
    )

    @pl.when((p == pl.num_programs(1) - 1) & (k == pl.num_programs(2) - 1))
    def _():
        o_ref[...] = acc_ref[...].astype(o_ref.dtype)


def masked_matmul_nn(a, w, mask, out_dtype):
    m = a.shape[0]
    planes, rows, cols = w.shape
    tk, tn = _tile(rows), _tile(cols)
    grid = (planes, cols // tn, rows // tk)
    return pl.pallas_call(
        _nn_kernel,
        grid=grid,
        in_specs=[
            pl.BlockSpec((m, tk), lambda p, j, k: (0, k)),
            pl.BlockSpec((None, tk, tn), lambda p, j, k: (p, k, j)),
            pl.BlockSpec((None, tk // BLOCK, 1, tn), lambda p, j, k: (p, k, 0, j)),
        ],
        out_specs=pl.BlockSpec((None, m, tn), lambda p, j, k: (p, 0, j)),
        out_shape=jax.ShapeDtypeStruct((planes, m, cols), out_dtype),
        scratch_shapes=[pltpu.VMEM((m, tn), jnp.float32), pltpu.VMEM((tk, tn), w.dtype)],
        compiler_params=pltpu.CompilerParams(
            dimension_semantics=("parallel", "parallel", "arbitrary"),
            vmem_limit_bytes=48 * 1024 * 1024,
        ),
        cost_estimate=pl.CostEstimate(
            flops=2 * m * planes * rows * cols,
            bytes_accessed=a.size * 2 * planes * (cols // tn) + w.size * 2
            + m * planes * cols * jnp.dtype(out_dtype).itemsize,
            transcendentals=0,
        ),
    )(a, w, mask)


def masked_matmul_nt(a, w, mask, out_dtype):
    planes, m, _ = a.shape
    _, rows, cols = w.shape
    tr, tk = _tile(rows), _tile(cols)
    grid = (rows // tr, planes, cols // tk)
    return pl.pallas_call(
        _nt_kernel,
        grid=grid,
        in_specs=[
            pl.BlockSpec((None, m, tk), lambda i, p, k: (p, 0, k)),
            pl.BlockSpec((None, tr, tk), lambda i, p, k: (p, i, k)),
            pl.BlockSpec((None, tr // BLOCK, 1, tk), lambda i, p, k: (p, i, 0, k)),
        ],
        out_specs=pl.BlockSpec((m, tr), lambda i, p, k: (0, i)),
        out_shape=jax.ShapeDtypeStruct((m, rows), out_dtype),
        scratch_shapes=[pltpu.VMEM((m, tr), jnp.float32), pltpu.VMEM((tr, tk), w.dtype)],
        compiler_params=pltpu.CompilerParams(
            dimension_semantics=("parallel", "arbitrary", "arbitrary"),
            vmem_limit_bytes=48 * 1024 * 1024,
        ),
        cost_estimate=pl.CostEstimate(
            flops=2 * m * planes * rows * cols,
            bytes_accessed=a.size * 2 * (rows // tr) + w.size * 2
            + m * rows * jnp.dtype(out_dtype).itemsize,
            transcendentals=0,
        ),
    )(a, w, mask)


def ring_gather(value, axis, work=None):
    count = lax.axis_size(axis)
    place = lax.axis_index(axis)
    step = [(index, (index + 1) % count) for index in range(count)]
    moving = value
    placed = jnp.zeros((count,) + value.shape, value.dtype)
    placed = lax.dynamic_update_index_in_dim(placed, value, place, 0)
    results = None
    if work is not None:
        done = work(value)
        results = jnp.zeros((done.shape[0], count) + done.shape[1:], done.dtype)
        results = lax.dynamic_update_index_in_dim(results, done, place, 1)
    for lap in range(1, count):
        moving = lax.ppermute(moving, axis, step)
        source = (place + count - lap) % count
        placed = lax.dynamic_update_index_in_dim(placed, moving, source, 0)
        if work is not None:
            results = lax.dynamic_update_index_in_dim(results, work(moving), source, 1)
    return placed, results


def ring_scatter(value, axis):
    count = lax.axis_size(axis)
    place = lax.axis_index(axis)
    step = [(index, (index + 1) % count) for index in range(count)]
    rows = value.shape[0] // count
    pieces = value.reshape((count, rows) + value.shape[1:])

    def piece(index):
        return lax.dynamic_index_in_dim(pieces, index % count, 0, False).astype(jnp.float32)

    running = piece(place + count - 1)
    for lap in range(1, count):
        arrived = lax.ppermute(running.astype(jnp.bfloat16), axis, step)
        running = arrived.astype(jnp.float32) + piece(place + 2 * count - 1 - lap)
    return running


class GatherRing:
    def __init__(self, value, axis):
        self.axis = axis
        self.count = lax.axis_size(axis)
        self.place = lax.axis_index(axis)
        self.step = [(index, (index + 1) % self.count) for index in range(self.count)]
        self.moving = value
        placed = jnp.zeros((self.count,) + value.shape, value.dtype)
        self.placed = lax.dynamic_update_index_in_dim(placed, value, self.place, 0)
        self.lap = 1

    def advance(self, tie=None):
        if self.lap >= self.count:
            return tie
        moved = lax.ppermute(self.moving, self.axis, self.step)
        if tie is not None:
            moved, tie = lax.optimization_barrier((moved, tie))
        source = (self.place + self.count - self.lap) % self.count
        self.placed = lax.dynamic_update_index_in_dim(self.placed, moved, source, 0)
        self.moving = moved
        self.lap += 1
        return tie

    def finish(self):
        while self.lap < self.count:
            self.advance()
        return self.placed


class ScatterRing:
    def __init__(self, value, axis):
        self.axis = axis
        self.count = lax.axis_size(axis)
        self.place = lax.axis_index(axis)
        self.step = [(index, (index + 1) % self.count) for index in range(self.count)]
        rows = value.shape[0] // self.count
        self.pieces = value.reshape((self.count, rows) + value.shape[1:])
        self.running = self.piece(self.place + self.count - 1)
        self.lap = 1

    def piece(self, index):
        return lax.dynamic_index_in_dim(
            self.pieces, index % self.count, 0, False
        ).astype(jnp.float32)

    def advance(self, tie=None):
        if self.lap >= self.count:
            return tie
        arrived = lax.ppermute(self.running.astype(jnp.bfloat16), self.axis, self.step)
        if tie is not None:
            arrived, tie = lax.optimization_barrier((arrived, tie))
        self.running = arrived.astype(jnp.float32) + self.piece(
            self.place + 2 * self.count - 1 - self.lap
        )
        self.lap += 1
        return tie

    def finish(self):
        while self.lap < self.count:
            self.advance()
        return self.running


def carried_in(value, axis, join, neutral):
    place = lax.axis_index(axis)
    gathered = lax.all_gather(value.astype(jnp.bfloat16), axis)
    state = jnp.zeros_like(value) + jnp.asarray(neutral, value.dtype)

    def carried_one(lap, state):
        return join(state, lax.dynamic_index_in_dim(gathered, lap, 0, False).astype(value.dtype))

    return lax.fori_loop(0, place, carried_one, state)


def entering(value, axis, join, neutral):
    count = lax.axis_size(axis)
    place = lax.axis_index(axis)
    ahead = count - 1 - place
    gathered = lax.all_gather(
        value.astype(jnp.bfloat16 if value.dtype == jnp.float32 else value.dtype), axis
    )
    state = jnp.zeros_like(value) + jnp.asarray(neutral, value.dtype)

    def entering_one(lap, state):
        source = count - 1 - lap
        return join(state, lax.dynamic_index_in_dim(gathered, source, 0, False).astype(value.dtype))

    return lax.fori_loop(0, ahead, entering_one, state)


def expand_blocks(blocks):
    row_blocks, col_blocks = blocks.shape
    spread = jnp.broadcast_to(
        blocks.astype(jnp.bfloat16)[:, None, :, None], (row_blocks, BLOCK, col_blocks, BLOCK)
    )
    return spread.reshape(row_blocks * BLOCK, col_blocks * BLOCK)


def qkv_keep_table(qkv_blocks):
    tables = [expand_blocks(qkv_blocks[projection]) for projection in range(3)]
    return jnp.stack(tables, axis=1)


def add_states(earlier, following):
    return earlier + following


def on_device(
    tokens, spike_query, spike_key, qkv_weight, qkv_blocks, out_weight, out_blocks, cotangent
):
    model_width = tokens.shape[1]
    block_rows = spike_query.shape[0]
    local_heads = spike_query.shape[1]
    features = qkv_weight.shape[2]
    head_width = features // local_heads
    row_blocks = model_width // BLOCK
    col_blocks = features // BLOCK
    highest = lax.Precision.HIGHEST
    qkv_planes = jnp.transpose(qkv_weight, (1, 0, 2))
    qkv_spread = jnp.broadcast_to(
        qkv_blocks.astype(jnp.bfloat16)[:, :, None, :, None],
        (3, row_blocks, 1, col_blocks, BLOCK),
    ).reshape(3, row_blocks, 1, features)
    out_planes = out_weight[None]
    out_spread = jnp.broadcast_to(
        out_blocks.astype(jnp.bfloat16)[None, :, None, :, None],
        (1, col_blocks, 1, row_blocks, BLOCK),
    ).reshape(1, col_blocks, 1, model_width)
    gathered, projected = ring_gather(
        tokens, "tp", lambda piece: masked_matmul_nn(piece, qkv_planes, qkv_spread, jnp.bfloat16)
    )
    gathered = gathered.reshape(block_rows, model_width)
    projected = projected.reshape(3, block_rows, features)
    projected, cotangent_late = lax.optimization_barrier((projected, cotangent))
    projected = projected.reshape(3, block_rows, local_heads, head_width)
    query_spikes = spike_query.astype(jnp.bfloat16)[:, :, None]
    key_spikes = spike_key.astype(jnp.bfloat16)[:, :, None]
    query_spiked = projected[0] * query_spikes
    key_spiked = projected[1] * key_spikes
    values = projected[2]
    query_wide = query_spiked.astype(jnp.float32)
    key_wide = key_spiked.astype(jnp.float32)
    local_state = jnp.einsum("shd,she->hde", key_spiked, values, preferred_element_type=jnp.float32)
    zeros_state = jnp.zeros_like(local_state)
    prior_state = carried_in(local_state, "ctx", add_states, zeros_state)
    positions = lax.iota(jnp.int32, block_rows)
    causal_keep = positions[:, None] >= positions[None, :]
    scores = jnp.einsum(
        "thd,shd->hts", query_spiked, key_spiked, preferred_element_type=jnp.float32
    )
    scores = jnp.where(causal_keep, scores, 0.0).astype(jnp.bfloat16)
    cotangent_ring = GatherRing(cotangent_late, "tp")
    scores = cotangent_ring.advance(scores)
    mixed_rows = jnp.einsum("hts,she->the", scores, values, preferred_element_type=jnp.float32)
    mixed_rows = mixed_rows + jnp.einsum("thd,hde->the", query_wide, prior_state, precision=highest)
    mixed_rows = cotangent_ring.advance(mixed_rows)
    inv_rms = lax.rsqrt(jnp.mean(mixed_rows * mixed_rows, axis=-1, keepdims=True) + EPSILON)
    normed = mixed_rows * inv_rms
    attended = normed.astype(jnp.bfloat16).reshape(block_rows, features)
    head_part = masked_matmul_nn(attended, out_planes, out_spread, jnp.bfloat16)[0]
    head_part = cotangent_ring.advance(head_part)
    grad_rows = cotangent_ring.finish().reshape(block_rows, model_width)
    head_part, grad_rows = lax.optimization_barrier((head_part, grad_rows))
    head_ring = ScatterRing(head_part, "tp")
    ctx_count = lax.axis_size("ctx")
    ctx_place = lax.axis_index("ctx")
    slice_rows = model_width // ctx_count
    slice_blocks = slice_rows // BLOCK
    norm_factor = 1.0 / math.sqrt(block_rows * ctx_count)
    out_part = jnp.einsum("tm,tf->mf", grad_rows, attended, preferred_element_type=jnp.float32)
    out_sum = lax.psum_scatter(
        out_part.astype(jnp.bfloat16), "ctx", scatter_dimension=0, tiled=True
    ).astype(jnp.float32)
    out_keep = lax.dynamic_slice_in_dim(out_blocks, ctx_place * slice_blocks, slice_blocks, 1)
    out_keep = jnp.broadcast_to(
        jnp.transpose(out_keep).astype(jnp.float32)[:, None, :, None],
        (slice_blocks, BLOCK, col_blocks, BLOCK),
    ).reshape(slice_rows, features)
    out_grad = jnp.transpose(out_sum * out_keep * norm_factor)
    grad_attended = masked_matmul_nt(grad_rows[None], out_planes, out_spread, jnp.float32)
    grad_attended = grad_attended.reshape(block_rows, local_heads, head_width)
    inner_mean = jnp.mean(grad_attended * normed, axis=-1, keepdims=True)
    grad_mixed = inv_rms * (grad_attended - normed * inner_mean)
    grad_low = grad_mixed.astype(jnp.bfloat16)
    local_adjoint = jnp.einsum("thd,the->hde", query_wide, grad_mixed, precision=highest)
    after_state = entering(local_adjoint, "ctx", add_states, zeros_state)
    adjoint_scores = jnp.einsum(
        "the,she->hts", grad_low, values, preferred_element_type=jnp.float32
    )
    adjoint_scores = jnp.where(causal_keep, adjoint_scores, 0.0).astype(jnp.bfloat16)
    adjoint_scores = head_ring.advance(adjoint_scores)
    grad_query = jnp.einsum(
        "hts,shd->thd", adjoint_scores, key_spiked, preferred_element_type=jnp.float32
    )
    grad_query = grad_query + jnp.einsum("the,hde->thd", grad_mixed, prior_state, precision=highest)
    grad_key = jnp.einsum(
        "hts,thd->shd", adjoint_scores, query_spiked, preferred_element_type=jnp.float32
    )
    grad_key = grad_key + jnp.einsum(
        "she,hde->shd", values.astype(jnp.float32), after_state, precision=highest
    )
    grad_value = jnp.einsum("hts,the->she", scores, grad_low, preferred_element_type=jnp.float32)
    grad_value = grad_value + jnp.einsum("shd,hde->she", key_wide, after_state, precision=highest)
    grad_proj = jnp.stack(
        [
            (grad_query * query_spikes.astype(jnp.float32)).astype(jnp.bfloat16),
            (grad_key * key_spikes.astype(jnp.float32)).astype(jnp.bfloat16),
            grad_value.astype(jnp.bfloat16),
        ],
        axis=0,
    ).reshape(3, block_rows, features)
    qkv_part = jnp.einsum("tm,ptc->mpc", gathered, grad_proj, preferred_element_type=jnp.float32)
    qkv_sum = lax.psum_scatter(
        qkv_part.astype(jnp.bfloat16), "ctx", scatter_dimension=0, tiled=True
    ).astype(jnp.float32)
    qkv_keep = lax.dynamic_slice_in_dim(qkv_blocks, ctx_place * slice_blocks, slice_blocks, 1)
    qkv_keep = jnp.broadcast_to(
        jnp.transpose(qkv_keep, (1, 0, 2)).astype(jnp.float32)[:, None, :, :, None],
        (slice_blocks, BLOCK, 3, col_blocks, BLOCK),
    ).reshape(slice_rows, 3, features)
    qkv_grad = qkv_sum * qkv_keep * norm_factor
    grad_proj = head_ring.advance(grad_proj)
    grad_proj_late = grad_proj
    token_sum = ring_scatter(
        masked_matmul_nt(grad_proj_late, qkv_planes, qkv_spread, jnp.bfloat16), "tp"
    )
    head_sum = head_ring.finish()
    layer_out = (tokens.astype(jnp.float32) + head_sum).astype(jnp.bfloat16)
    token_grad = (cotangent.astype(jnp.float32) + token_sum).astype(jnp.bfloat16)
    return (layer_out, token_grad, qkv_grad, out_grad)


def solution(mesh):
    placed = (
        P(("ctx", "tp"), None),
        P("ctx", "tp"),
        P("ctx", "tp"),
        P(None, None, "tp"),
        P(None, None, "tp"),
        P("tp", None),
        P("tp", None),
        P(("ctx", "tp"), None),
    )
    return jax.shard_map(
        on_device,
        mesh=mesh,
        in_specs=placed,
        out_specs=(
            P(("ctx", "tp"), None),
            P(("ctx", "tp"), None),
            P("ctx", None, "tp"),
            P("tp", "ctx"),
        ),
        check_vma=False,
    )
```

profile of v0, /device:TPU:0, one launch (start us, length us, event | category | flops | bytes accessed | tf_op | source)
XLA Modules:
  0.0 487.9 jit_solution(14450327088689544676)
XLA Ops:
  16.7 14.0 %shard_map.111 = bf16[3,128,1024]{2,1,0:T(8,128)(2,1)S(1)} custom-call(bf16[128,4096]{1,0:T(8,128)(2,1)S(1)} %copy-done, bf16[3,4096,1024]{2,1,0:T(8,128)(2,1)} %bitcast.140, bf16[3,32,1,1024]{3,2,1,0:T(2,128)(2,1)S(1)} %broadcast_in_dim.120.m_ref), custom_call_target="tpu_custom_call" | custom-call | flops 3221225472 | bytes 29097984 | tf_op jit(solution)/shard_map/pallas_call | solution.py:66
  37.1 24.7 %collective-permute-done.1.a_ref = bf16[128,4096]{1,0:T(8,128)(2,1)S(1)} collective-permute-done((bf16[128,4096]{1,0:T(8,128)(2,1)S(1)}, bf16[128,4096]{1,0:T(8,128)(2,1)S(1)}, u32[]{:S(2)}, u32[]{:S(2)}) %collective-permute-start.1) | collective-permute-done | bytes 1048608 | tf_op jit(solution)/shard_map/ppermute | solution.py:132
  61.8 14.0 %shard_map.112 = bf16[3,128,1024]{2,1,0:T(8,128)(2,1)S(1)} custom-call(bf16[128,4096]{1,0:T(8,128)(2,1)S(1)} %collective-permute-done.a_ref, bf16[3,4096,1024]{2,1,0:T(8,128)(2,1)} %bitcast.141, bf16[3,32,1,1024]{3,2,1,0:T(2,128)(2,1)S(1)} %broadcast_in_dim.120.m_ref), custom_call_target="tpu_custom_call" | custom-call | flops 3221225472 | bytes 29097984 | tf_op jit(solution)/shard_map/pallas_call | solution.py:66
  75.9 14.0 %shard_map.113 = bf16[3,128,1024]{2,1,0:T(8,128)(2,1)S(1)} custom-call(bf16[128,4096]{1,0:T(8,128)(2,1)S(1)} %collective-permute-done.1.a_ref, bf16[3,4096,1024]{2,1,0:T(8,128)(2,1)} %bitcast.142, bf16[3,32,1,1024]{3,2,1,0:T(2,128)(2,1)S(1)} %broadcast_in_dim.120.m_ref), custom_call_target="tpu_custom_call" | custom-call | flops 3221225472 | bytes 29097984 | tf_op jit(solution)/shard_map/pallas_call | solution.py:66
  90.0 14.0 %shard_map.114 = bf16[3,128,1024]{2,1,0:T(8,128)(2,1)S(1)} custom-call(bf16[128,4096]{1,0:T(8,128)(2,1)S(1)} %collective-permute-done.2.a_ref, bf16[3,4096,1024]{2,1,0:T(8,128)(2,1)} %bitcast.143, bf16[3,32,1,1024]{3,2,1,0:T(2,128)(2,1)S(1)} %broadcast_in_dim.120.m_ref), custom_call_target="tpu_custom_call" | custom-call | flops 3221225472 | bytes 29097984 | tf_op jit(solution)/shard_map/pallas_call | solution.py:66
  116.9 4.6 select_convert_fusion.1
  125.1 17.3 %collective-permute-done.3 = bf16[128,4096]{1,0:T(8,128)(2,1)} collective-permute-done((bf16[128,4096]{1,0:T(8,128)(2,1)}, bf16[128,4096]{1,0:T(8,128)(2,1)}, u32[]{:S(2)}, u32[]{:S(2)}) %collective-permute-start.3) | collective-permute-done | bytes 1048608 | tf_op jit(solution)/shard_map/ppermute | solution.py:171
  149.9 17.1 %collective-permute-done.4 = bf16[128,4096]{1,0:T(8,128)(2,1)} collective-permute-done((bf16[128,4096]{1,0:T(8,128)(2,1)}, bf16[128,4096]{1,0:T(8,128)(2,1)}, u32[]{:S(2)}, u32[]{:S(2)}) %collective-permute-start.4) | collective-permute-done | bytes 1048608 | tf_op jit(solution)/shard_map/ppermute | solution.py:171
  170.3 7.3 %shard_map.115 = bf16[1,512,4096]{2,1,0:T(8,128)(2,1)S(1)} custom-call(bf16[512,1024]{1,0:T(8,128)(2,1)S(1)} %copy.122.a_ref, bf16[1,1024,4096]{2,1,0:T(8,128)(2,1)} %bitcast.172, bf16[1,8,1,4096]{3,2,1,0:T(2,128)(2,1)S(1)} %copy-done.3), custom_call_target="tpu_custom_call" | custom-call | flops 4294967296 | bytes 16777216 | tf_op jit(solution)/shard_map/pallas_call | solution.py:66
  180.7 13.2 %collective-permute-done.5 = bf16[128,4096]{1,0:T(8,128)(2,1)S(1)} collective-permute-done((bf16[128,4096]{1,0:T(8,128)(2,1)}, bf16[128,4096]{1,0:T(8,128)(2,1)S(1)}, u32[]{:S(2)}, u32[]{:S(2)}) %collective-permute-start.5) | collective-permute-done | bytes 1048608 | tf_op jit(solution)/shard_map/ppermute | solution.py:171
  195.4 8.2 %shard_map.116 = f32[512,1024]{1,0:T(8,128)S(1)} custom-call(bf16[1,512,4096]{2,1,0:T(8,128)(2,1)} %bitcast.27.a_ref, bf16[1,1024,4096]{2,1,0:T(8,128)(2,1)} %bitcast.173, bf16[1,8,1,4096]{3,2,1,0:T(2,128)(2,1)S(1)} %copy-done.3), custom_call_target="tpu_custom_call" | custom-call | flops 4294967296 | bytes 14680064 | tf_op jit(solution)/shard_map/pallas_call | solution.py:95
  212.1 9.2 %convolution_convert_fusion.1 = bf16[4096,1024]{1,0:T(8,128)(2,1)} fusion(bf16[512,4096]{1,0:T(8,128)(2,1)} %bitcast.24, bf16[512,1024]{0,1:T(8,128)(2,1)S(1)} %bitcast.165), kind=kOutput, calls=%fused_computation.5 | convolution fusion | flops 4299161600 | bytes 13631488 | tf_op jit(solution)/shard_map/tm,tf->mf/dot_general | solution.py:326
  227.0 19.5 %collective-permute-done.6 = bf16[128,4096]{1,0:T(8,128)(2,1)} collective-permute-done((bf16[128,4096]{1,0:T(8,128)(2,1)}, bf16[128,4096]{1,0:T(8,128)(2,1)}, u32[]{:S(2)}, u32[]{:S(2)}) %collective-permute-start.6) | collective-permute-done | bytes 1048608 | tf_op jit(solution)/shard_map/ppermute | solution.py:205
  249.5 8.1 %while.23 = (s32[]{:T(128)}, f32[8,128,128]{2,1,0:T(8,128)S(1)}, s32[]{:T(128)}, bf16[8,8,128,128]{3,2,1,0:T(8,128)(2,1)}, s32[]{:T(128)}, /*index=5*/s32[]{:T(128)}, s32[]{:T(128)}, s32[]{:T(128)}) while((s32[]{:T(128)}, f32[8,128,128]{2,1,0:T(8,128)S(1)}, s32[]{:T(128)}, bf16[8,8,128,128]{3,2,1,0:T(8,128)(2,1)}, s32[]{:T(128)}, ...), condition=%wide.region_5.6_spmd, body=%wide.region_4.5_spmd.sunk | while | flops 262150 | bytes 1310863 | solution.py:244
  272.3 20.9 %convolution_convert_fusion = bf16[4096,3,1024]{2,0,1:T(8,128)(2,1)} fusion(bf16[512,4096,1]{1,0,2:T(8,128)(2,1)} %bitcast.169, bf16[1,512,1024]{2,1,0:T(8,128)(2,1)} %copy.125, bf16[1,512,1024]{2,1,0:T(8,128)(2,1)S(1)} %copy.124, bf16[1,512,1024]{2,1,0:T(8,128)(2,1)S(1)} %copy-done.21), kind=kOutput, calls=%fused_computation.2 | convolution fusion | flops 12906921984 | bytes 32505856 | tf_op jit(solution)/shard_map/tm,ptc->mpc/dot_general | solution.py:368
  295.9 21.0 %collective-permute-done.7 = bf16[128,4096]{1,0:T(8,128)(2,1)S(1)} collective-permute-done((bf16[128,4096]{1,0:T(8,128)(2,1)S(1)}, bf16[128,4096]{1,0:T(8,128)(2,1)S(1)}, u32[]{:S(2)}, u32[]{:S(2)}) %collective-permute-start.7) | collective-permute-done | bytes 1048608 | tf_op jit(solution)/shard_map/ppermute | solution.py:205
  316.9 24.6 %shard_map.117 = bf16[512,4096]{1,0:T(8,128)(2,1)} custom-call(bf16[3,512,1024]{2,1,0:T(8,128)(2,1)S(1)} %pad_maximum_fusion.a_ref, bf16[3,4096,1024]{2,1,0:T(8,128)(2,1)} %bitcast.144, bf16[3,32,1,1024]{3,2,1,0:T(2,128)(2,1)S(1)} %broadcast_in_dim.120.m_ref), custom_call_target="tpu_custom_call" | custom-call | flops 12884901888 | bytes 41943040 | tf_op jit(solution)/shard_map/pallas_call | solution.py:95
  343.2 21.8 %collective-permute-done.9 = bf16[128,4096]{1,0:T(8,128)(2,1)S(1)} collective-permute-done((bf16[128,4096]{1,0:T(8,128)(2,1)S(1)}, bf16[128,4096]{1,0:T(8,128)(2,1)S(1)}, u32[]{:S(2)}, u32[]{:S(2)}) %collective-permute-start.9) | collective-permute-done | bytes 1048608 | tf_op jit(solution)/shard_map/ppermute | solution.py:152
  369.2 25.2 %collective-permute-done.10 = bf16[128,4096]{1,0:T(8,128)(2,1)} collective-permute-done((bf16[128,4096]{1,0:T(8,128)(2,1)S(1)}, bf16[128,4096]{1,0:T(8,128)(2,1)}, u32[]{:S(2)}, u32[]{:S(2)}) %collective-permute-start.10) | collective-permute-done | bytes 1048608 | tf_op jit(solution)/shard_map/ppermute | solution.py:152
  400.6 7.3 %reshape.106 = f32[512,3,1024]{2,0,1:T(8,128)} reshape(f32[4,128,3,8,128]{4,3,1,0,2:T(8,128)} %broadcast_in_dim.118) | data formatting | bytes 12582912 | tf_op jit(solution)/shard_map/reshape | solution.py:376
  407.8 9.0 %collective-permute-done.8 = bf16[128,4096]{1,0:T(8,128)(2,1)S(1)} collective-permute-done((bf16[128,4096]{1,0:T(8,128)(2,1)}, bf16[128,4096]{1,0:T(8,128)(2,1)S(1)}, u32[]{:S(2)}, u32[]{:S(2)}) %collective-permute-start.8) | collective-permute-done | bytes 1048608 | tf_op jit(solution)/shard_map/ppermute | solution.py:205
  419.6 9.8 %collective-permute-done.11 = bf16[128,4096]{1,0:T(8,128)(2,1)} collective-permute-done((bf16[128,4096]{1,0:T(8,128)(2,1)}, bf16[128,4096]{1,0:T(8,128)(2,1)}, u32[]{:S(2)}, u32[]{:S(2)}) %collective-permute-start.11) | collective-permute-done | bytes 1048608 | tf_op jit(solution)/shard_map/ppermute | solution.py:152
  436.4 36.5 %reduce-scatter.3.cloned.1.call-done = bf16[512,3,1024]{2,0,1:T(8,128)(2,1)} async-done(((bf16[4096,3,1024]{2,0,1:T(8,128)(2,1)}), bf16[512,3,1024]{2,0,1:T(8,128)(2,1)}) %reduce-scatter.3.cloned.1.call-update) | async-done | bytes 3145744 | tf_op jit(solution)/shard_map/reduce_scatter | solution.py:369
  472.9 8.0 %multiply_multiply_fusion = f32[512,3,1024]{2,0,1:T(8,128)} fusion(f32[512,3,1024]{2,0,1:T(8,128)} %reshape.106, bf16[512,3,1024]{2,0,1:T(8,128)(2,1)} %reduce-scatter.3.cloned.1.call-done), kind=kLoop, calls=%fused_computation.6 | loop fusion | flops 4718592 | bytes 15728640 | tf_op jit(solution)/shard_map/mul | solution.py:377
  (174 shorter events, 111.5 us)
Async XLA Ops:
  7.2 137.6 %all-gather.5.cloned.1.call-start = ((), (), s32[]{:S(2)}) async-start(), calls=%async_computation.4 | async-start | bytes 2359296 | tf_op jit(solution)/shard_map/all_gather | solution.py:222
  7.2 28.5 %collective-permute-start = (bf16[128,4096]{1,0:T(8,128)(2,1)}, bf16[128,4096]{1,0:T(8,128)(2,1)S(1)}, u32[]{:S(2)}, u32[]{:S(2)}) collective-permute-start(bf16[128,4096]{1,0:T(8,128)(2,1)} %a_ref.1), channel_id=1, source_target_pairs={{0,1},{1,2},{2,3},{3,0},{4,5},{5,6},{6,7},{7,4},{8,9},{9,10},{10,1... | collective-permute-start | bytes 3145736 | tf_op jit(solution)/shard_map/ppermute | solution.py:132
  14.2 130.6 %copy-start.28 = (bf16[512,8]{0,1:T(8,128)(2,1)}, bf16[512,8]{0,1:T(8,128)(2,1)S(1)}, u32[]{:S(2)}) copy-start(bf16[512,8]{0,1:T(8,128)(2,1)S(1)} %get-tuple-element.142) | copy-start | bytes 24580
  15.5 101.3 %copy-start.31 = (bf16[512,8]{0,1:T(8,128)(2,1)}, bf16[512,8]{0,1:T(8,128)(2,1)S(1)}, u32[]{:S(2)}) copy-start(bf16[512,8]{0,1:T(8,128)(2,1)S(1)} %get-tuple-element.144) | copy-start | bytes 24580
  35.7 26.1 %collective-permute-start.1 = (bf16[128,4096]{1,0:T(8,128)(2,1)S(1)}, bf16[128,4096]{1,0:T(8,128)(2,1)S(1)}, u32[]{:S(2)}, u32[]{:S(2)}) collective-permute-start(bf16[128,4096]{1,0:T(8,128)(2,1)S(1)} %collective-permute-done.a_ref), channel_id=1, source_target_pairs={{0,1},{1,2},{2,3},{3,0},{4,5},{5,6},{6,7},{7,4},{8,9},{9,10},{10,1... | collective-permute-start | bytes 3145736 | tf_op jit(solution)/shard_map/ppermute | solution.py:132
  37.1 38.7 %copy-start.20 = (bf16[4,128,4096]{2,1,0:T(8,128)(2,1)}, bf16[4,128,4096]{2,1,0:T(8,128)(2,1)S(1)}, u32[]{:S(2)}) copy-start(bf16[4,128,4096]{2,1,0:T(8,128)(2,1)S(1)} %bitcast_dynamic-update-slice_fusion.3) | copy-start | bytes 12582916
  61.8 28.2 %collective-permute-start.2 = (bf16[128,4096]{1,0:T(8,128)(2,1)S(1)}, bf16[128,4096]{1,0:T(8,128)(2,1)S(1)}, u32[]{:S(2)}, u32[]{:S(2)}) collective-permute-start(bf16[128,4096]{1,0:T(8,128)(2,1)S(1)} %collective-permute-done.1.a_ref), channel_id=1, source_target_pairs={{0,1},{1,2},{2,3},{3,0},{4,5},{5,6},{6,7},{7,4},{8,9},{9,10},{10,1... | collective-permute-start | bytes 3145736 | tf_op jit(solution)/shard_map/ppermute | solution.py:132
  113.1 136.3 %all-gather.7.cloned.1.call-start = ((), (), s32[]{:S(2)}) async-start(), calls=%async_computation.5 | async-start | bytes 2359296 | tf_op jit(solution)/shard_map/all_gather | solution.py:235
  116.8 28.1 %copy-start.10 = (bf16[1,512,1024]{1,2,0:T(8,128)(2,1)}, bf16[1,512,1024]{1,2,0:T(8,128)(2,1)S(1)}, u32[]{:S(2)}) copy-start(bf16[1,512,1024]{1,2,0:T(8,128)(2,1)S(1)} %copy.121) | copy-start | bytes 3145732
  116.8 25.6 %collective-permute-start.3 = (bf16[128,4096]{1,0:T(8,128)(2,1)}, bf16[128,4096]{1,0:T(8,128)(2,1)}, u32[]{:S(2)}, u32[]{:S(2)}) collective-permute-start(bf16[128,4096]{1,0:T(8,128)(2,1)} %param.19), channel_id=1, source_target_pairs={{0,1},{1,2},{2,3},{3,0},{4,5},{5,6},{6,7},{7,4},{8,9},{9,10},{10,1... | collective-permute-start | bytes 3145736 | tf_op jit(solution)/shard_map/ppermute | solution.py:171
  142.4 24.6 %collective-permute-start.4 = (bf16[128,4096]{1,0:T(8,128)(2,1)}, bf16[128,4096]{1,0:T(8,128)(2,1)}, u32[]{:S(2)}, u32[]{:S(2)}) collective-permute-start(bf16[128,4096]{1,0:T(8,128)(2,1)} %collective-permute-done.3), channel_id=1, source_target_pairs={{0,1},{1,2},{2,3},{3,0},{4,5},{5,6},{6,7},{7,4},{8,9},{9,10},{10,1... | collective-permute-start | bytes 3145736 | tf_op jit(solution)/shard_map/ppermute | solution.py:171
  170.1 23.8 %collective-permute-start.5 = (bf16[128,4096]{1,0:T(8,128)(2,1)}, bf16[128,4096]{1,0:T(8,128)(2,1)S(1)}, u32[]{:S(2)}, u32[]{:S(2)}) collective-permute-start(bf16[128,4096]{1,0:T(8,128)(2,1)} %collective-permute-done.4), channel_id=1, source_target_pairs={{0,1},{1,2},{2,3},{3,0},{4,5},{5,6},{6,7},{7,4},{8,9},{9,10},{10,1... | collective-permute-start | bytes 3145736 | tf_op jit(solution)/shard_map/ppermute | solution.py:171
  212.1 220.4 %reduce-scatter.5.cloned.1.call-start = ((), (), s32[]{:S(2)}) async-start(), calls=%async_computation.3 | async-start | bytes 9437184 | tf_op jit(solution)/shard_map/reduce_scatter | solution.py:327
  221.3 251.6 %reduce-scatter.3.cloned.1.call-start = ((), (), s32[]{:S(2)}) async-start(), calls=%async_computation.2 | async-start | bytes 28311552 | tf_op jit(solution)/shard_map/reduce_scatter | solution.py:369
  223.7 22.9 %collective-permute-start.6 = (bf16[128,4096]{1,0:T(8,128)(2,1)}, bf16[128,4096]{1,0:T(8,128)(2,1)}, u32[]{:S(2)}, u32[]{:S(2)}) collective-permute-start(bf16[128,4096]{1,0:T(8,128)(2,1)} %dynamic-slice_bitcast_fusion.1), channel_id=1, source_target_pairs={{0,1},{1,2},{2,3},{3,0},{4,5},{5,6},{6,7},{7,4},{8,9},{9,10},{10,1... | collective-permute-start | bytes 3145736 | tf_op jit(solution)/shard_map/ppermute | solution.py:205
  295.2 21.7 %collective-permute-start.7 = (bf16[128,4096]{1,0:T(8,128)(2,1)S(1)}, bf16[128,4096]{1,0:T(8,128)(2,1)S(1)}, u32[]{:S(2)}, u32[]{:S(2)}) collective-permute-start(bf16[128,4096]{1,0:T(8,128)(2,1)S(1)} %fusion.9), channel_id=1, source_target_pairs={{0,1},{1,2},{2,3},{3,0},{4,5},{5,6},{6,7},{7,4},{8,9},{9,10},{10,1... | collective-permute-start | bytes 3145736 | tf_op jit(solution)/shard_map/ppermute | solution.py:205
  316.9 24.6 %copy-start.25 = (bf16[128,4096]{1,0:T(8,128)(2,1)}, bf16[128,4096]{1,0:T(8,128)(2,1)S(1)}, u32[]{:S(2)}) copy-start(bf16[128,4096]{1,0:T(8,128)(2,1)S(1)} %collective-permute-done.7) | copy-start | bytes 3145732
  341.4 25.1 %copy-start.35 = (s32[8,32]{1,0:T(8,128)S(1)}, s32[8,32]{1,0:T(8,128)}, u32[]{:S(2)}) copy-start(s32[8,32]{1,0:T(8,128)} %param.18) | copy-start | bytes 3076
  341.4 25.2 %copy-start.26 = (bf16[128,4096]{1,0:T(8,128)(2,1)S(1)}, bf16[128,4096]{1,0:T(8,128)(2,1)}, u32[]{:S(2)}) copy-start(bf16[128,4096]{1,0:T(8,128)(2,1)} %copy-done.25) | copy-start | bytes 3145732
  343.1 21.8 %collective-permute-start.9 = (bf16[128,4096]{1,0:T(8,128)(2,1)S(1)}, bf16[128,4096]{1,0:T(8,128)(2,1)S(1)}, u32[]{:S(2)}, u32[]{:S(2)}) collective-permute-start(bf16[128,4096]{1,0:T(8,128)(2,1)S(1)} %dynamic-slice_bitcast_fusion), channel_id=1, source_target_pairs={{0,1},{1,2},{2,3},{3,0},{4,5},{5,6},{6,7},{7,4},{8,9},{9,10},{10,1... | collective-permute-start | bytes 3145736 | tf_op jit(solution)/shard_map/ppermute | solution.py:152
  366.4 28.1 %collective-permute-start.10 = (bf16[128,4096]{1,0:T(8,128)(2,1)S(1)}, bf16[128,4096]{1,0:T(8,128)(2,1)}, u32[]{:S(2)}, u32[]{:S(2)}) collective-permute-start(bf16[128,4096]{1,0:T(8,128)(2,1)S(1)} %fusion.5), channel_id=1, source_target_pairs={{0,1},{1,2},{2,3},{3,0},{4,5},{5,6},{6,7},{7,4},{8,9},{9,10},{10,1... | collective-permute-start | bytes 3145736 | tf_op jit(solution)/shard_map/ppermute | solution.py:152
  366.6 30.6 %copy-start.34 = (s32[3,32,8]{1,2,0:T(8,128)S(1)}, s32[3,32,8]{1,2,0:T(8,128)}, u32[]{:S(2)}) copy-start(s32[3,32,8]{1,2,0:T(8,128)} %param.16) | copy-start | bytes 9220
  369.2 47.6 %collective-permute-start.8 = (bf16[128,4096]{1,0:T(8,128)(2,1)}, bf16[128,4096]{1,0:T(8,128)(2,1)S(1)}, u32[]{:S(2)}, u32[]{:S(2)}) collective-permute-start(bf16[128,4096]{1,0:T(8,128)(2,1)} %fusion.8), channel_id=1, source_target_pairs={{0,1},{1,2},{2,3},{3,0},{4,5},{5,6},{6,7},{7,4},{8,9},{9,10},{10,1... | collective-permute-start | bytes 3145736 | tf_op jit(solution)/shard_map/ppermute | solution.py:205
  397.2 32.2 %collective-permute-start.11 = (bf16[128,4096]{1,0:T(8,128)(2,1)}, bf16[128,4096]{1,0:T(8,128)(2,1)}, u32[]{:S(2)}, u32[]{:S(2)}) collective-permute-start(bf16[128,4096]{1,0:T(8,128)(2,1)} %fusion.4), channel_id=1, source_target_pairs={{0,1},{1,2},{2,3},{3,0},{4,5},{5,6},{6,7},{7,4},{8,9},{9,10},{10,1... | collective-permute-start | bytes 3145736 | tf_op jit(solution)/shard_map/ppermute | solution.py:152
  (28 other events, 232.3 us)
Sparse Core Ops, SparseCore 0:
  113.2 29.1 all-gather.4
  212.2 25.0 all-gather.6
  240.7 71.2 reduce-scatter.4
  316.0 156.8 reduce-scatter.2
where the time goes:
time: 498 us; the launch traced here: 488 us
  waiting for transfers between devices  220 us (44%)
  Pallas kernels  96 us (19%)
  matrix products  60.4 us (12%)
  local copies, waits for them, and re-layouts  49.9 us (10%)
  other arithmetic  42.6 us (9%)
  between operations  14.9 us (3%)
    pallas_call x5, Pallas kernels, masked_matmul_nn(): pl.pallas_call(_nn_kernel, grid=grid, in_specs=[pl.BlockSpec((m, tk), lam...  63.2 us
    ppermute x3, waiting for transfers between devices, ring_scatter(): arrived = lax.ppermute(running.astype(jnp.bfloat16), axis, step)  56.8 us
    ppermute x3, waiting for transfers between devices, advance(): lax.ppermute(self.running.astype(jnp.bfloat16), self.axis, self.step)  49.5 us
    ppermute x3, waiting for transfers between devices, advance(): moved = lax.ppermute(self.moving, self.axis, self.step)  47.6 us
    reduce_scatter x1, waiting for transfers between devices, on_device(): lax.psum_scatter(qkv_part.astype(jnp.bfloat16), 'ctx', scatter_dimension=...  36.5 us
    pallas_call x2, Pallas kernels, masked_matmul_nt(): pl.pallas_call(_nt_kernel, grid=grid, in_specs=[pl.BlockSpec((None, m, tk...  32.8 us
    ppermute x3, waiting for transfers between devices, ring_gather(): moving = lax.ppermute(moving, axis, step)  29.2 us
    dot_general x1, matrix products, on_device(): jnp.einsum('tm,ptc->mpc', gathered, grad_proj, preferred_element_type=jnp...  20.9 us
  transfers between devices with their start and end apart: 16, of which 12 were waited for; matrix products, arithmetic and copies ran while one was open for 25% of the time, Pallas kernels for 15%

commit v1 on v0

--- a/solution.py
+++ b/solution.py
@@ -344,7 +344,6 @@
         "the,she->hts", grad_low, values, preferred_element_type=jnp.float32
     )
     adjoint_scores = jnp.where(causal_keep, adjoint_scores, 0.0).astype(jnp.bfloat16)
-    adjoint_scores = head_ring.advance(adjoint_scores)
     grad_query = jnp.einsum(
         "hts,shd->thd", adjoint_scores, key_spiked, preferred_element_type=jnp.float32
     )
@@ -375,7 +374,6 @@
         (slice_blocks, BLOCK, 3, col_blocks, BLOCK),
     ).reshape(slice_rows, 3, features)
     qkv_grad = qkv_sum * qkv_keep * norm_factor
-    grad_proj = head_ring.advance(grad_proj)
     grad_proj_late = grad_proj
     token_sum = ring_scatter(
         masked_matmul_nt(grad_proj_late, qkv_planes, qkv_spread, jnp.bfloat16), "tp"

time: 498 us -> 498 us (level)
  waiting for transfers between devices: 220 us -> 202 us
  loops' own time: 0.39 us -> 8.81 us
  matrix products: 60.4 us -> 66.5 us
    ppermute x3, waiting for transfers between devices: 49.5 us -> 28.8 us  [advance(): lax.ppermute(self.running.astype(jnp.bfloat16), self.axis, self.step)]
    another operation x1, loops' own time: 0.38 us -> 8.79 us  [entering(): return lax.fori_loop(0, ahead, entering_one, state)]
  transfers between devices with their start and end apart: 16 -> 16, of which waited for: 12 -> 13; matrix products, arithmetic and copies ran while one was open for 25% -> 27% of each run, Pallas kernels for 15% -> 15%
where the time goes in v1:
time: 498 us; the launch traced here: 488 us
  waiting for transfers between devices  202 us (41%)
  Pallas kernels  93 us (19%)
  matrix products  66.5 us (13%)
  local copies, waits for them, and re-layouts  51.3 us (10%)
  other arithmetic  43.8 us (9%)
  between operations  14.5 us (3%)
  loops' own time  8.81 us (2%)
  starting transfers between devices  7.99 us (2%)
    pallas_call x5, Pallas kernels, masked_matmul_nn(): pl.pallas_call(_nn_kernel, grid=grid, in_specs=[pl.BlockSpec((m, tk), lam...  63.3 us
    ppermute x3, waiting for transfers between devices, ring_scatter(): arrived = lax.ppermute(running.astype(jnp.bfloat16), axis, step)  61.1 us
    ppermute x3, waiting for transfers between devices, advance(): moved = lax.ppermute(self.moving, self.axis, self.step)  47.5 us
    reduce_scatter x1, waiting for transfers between devices, on_device(): lax.psum_scatter(qkv_part.astype(jnp.bfloat16), 'ctx', scatter_dimension=...  34.6 us
    pallas_call x2, Pallas kernels, masked_matmul_nt(): pl.pallas_call(_nt_kernel, grid=grid, in_specs=[pl.BlockSpec((None, m, tk...  29.8 us
    ppermute x3, waiting for transfers between devices, ring_gather(): moving = lax.ppermute(moving, axis, step)  29.2 us
    ppermute x3, waiting for transfers between devices, advance(): lax.ppermute(self.running.astype(jnp.bfloat16), self.axis, self.step)  28.8 us
    dot_general x1, matrix products, on_device(): jnp.einsum('tm,ptc->mpc', gathered, grad_proj, preferred_element_type=jnp...  21.1 us
  transfers between devices with their start and end apart: 16, of which 13 were waited for; matrix products, arithmetic and copies ran while one was open for 27% of the time, Pallas kernels for 15%

profile of v1, /device:TPU:0, one launch (start us, length us, event | category | flops | bytes accessed | tf_op | source)
XLA Modules:
  0.0 487.9 jit_solution(3025844816437066768)
XLA Ops:
  16.7 14.0 %shard_map.111 = bf16[3,128,1024]{2,1,0:T(8,128)(2,1)S(1)} custom-call(bf16[128,4096]{1,0:T(8,128)(2,1)S(1)} %copy-done, bf16[3,4096,1024]{2,1,0:T(8,128)(2,1)} %bitcast.140, bf16[3,32,1,1024]{3,2,1,0:T(2,128)(2,1)S(1)} %broadcast_in_dim.120.m_ref), custom_call_target="tpu_custom_call" | custom-call | flops 3221225472 | bytes 29097984 | tf_op jit(solution)/shard_map/pallas_call | solution.py:66
  31.2 4.5 collective-permute-done.a_ref
  37.1 24.7 %collective-permute-done.1.a_ref = bf16[128,4096]{1,0:T(8,128)(2,1)S(1)} collective-permute-done((bf16[128,4096]{1,0:T(8,128)(2,1)S(1)}, bf16[128,4096]{1,0:T(8,128)(2,1)S(1)}, u32[]{:S(2)}, u32[]{:S(2)}) %collective-permute-start.1) | collective-permute-done | bytes 1048608 | tf_op jit(solution)/shard_map/ppermute | solution.py:132
  61.8 14.0 %shard_map.112 = bf16[3,128,1024]{2,1,0:T(8,128)(2,1)S(1)} custom-call(bf16[128,4096]{1,0:T(8,128)(2,1)S(1)} %collective-permute-done.a_ref, bf16[3,4096,1024]{2,1,0:T(8,128)(2,1)} %bitcast.141, bf16[3,32,1,1024]{3,2,1,0:T(2,128)(2,1)S(1)} %broadcast_in_dim.120.m_ref), custom_call_target="tpu_custom_call" | custom-call | flops 3221225472 | bytes 29097984 | tf_op jit(solution)/shard_map/pallas_call | solution.py:66
  75.9 14.0 %shard_map.113 = bf16[3,128,1024]{2,1,0:T(8,128)(2,1)S(1)} custom-call(bf16[128,4096]{1,0:T(8,128)(2,1)S(1)} %collective-permute-done.1.a_ref, bf16[3,4096,1024]{2,1,0:T(8,128)(2,1)} %bitcast.142, bf16[3,32,1,1024]{3,2,1,0:T(2,128)(2,1)S(1)} %broadcast_in_dim.120.m_ref), custom_call_target="tpu_custom_call" | custom-call | flops 3221225472 | bytes 29097984 | tf_op jit(solution)/shard_map/pallas_call | solution.py:66
  90.0 14.0 %shard_map.114 = bf16[3,128,1024]{2,1,0:T(8,128)(2,1)S(1)} custom-call(bf16[128,4096]{1,0:T(8,128)(2,1)S(1)} %collective-permute-done.2.a_ref, bf16[3,4096,1024]{2,1,0:T(8,128)(2,1)} %bitcast.143, bf16[3,32,1,1024]{3,2,1,0:T(2,128)(2,1)S(1)} %broadcast_in_dim.120.m_ref), custom_call_target="tpu_custom_call" | custom-call | flops 3221225472 | bytes 29097984 | tf_op jit(solution)/shard_map/pallas_call | solution.py:66
  116.9 4.6 select_convert_fusion.1
  125.1 17.3 %collective-permute-done.3 = bf16[128,4096]{1,0:T(8,128)(2,1)} collective-permute-done((bf16[128,4096]{1,0:T(8,128)(2,1)}, bf16[128,4096]{1,0:T(8,128)(2,1)}, u32[]{:S(2)}, u32[]{:S(2)}) %collective-permute-start.3) | collective-permute-done | bytes 1048608 | tf_op jit(solution)/shard_map/ppermute | solution.py:171
  150.0 17.1 %collective-permute-done.4 = bf16[128,4096]{1,0:T(8,128)(2,1)} collective-permute-done((bf16[128,4096]{1,0:T(8,128)(2,1)}, bf16[128,4096]{1,0:T(8,128)(2,1)}, u32[]{:S(2)}, u32[]{:S(2)}) %collective-permute-start.4) | collective-permute-done | bytes 1048608 | tf_op jit(solution)/shard_map/ppermute | solution.py:171
  170.4 7.3 %shard_map.115 = bf16[1,512,4096]{2,1,0:T(8,128)(2,1)S(1)} custom-call(bf16[512,1024]{1,0:T(8,128)(2,1)S(1)} %copy.122.a_ref, bf16[1,1024,4096]{2,1,0:T(8,128)(2,1)} %bitcast.172, bf16[1,8,1,4096]{3,2,1,0:T(2,128)(2,1)S(1)} %copy-done.3), custom_call_target="tpu_custom_call" | custom-call | flops 4294967296 | bytes 16777216 | tf_op jit(solution)/shard_map/pallas_call | solution.py:66
  180.8 13.2 %collective-permute-done.5 = bf16[128,4096]{1,0:T(8,128)(2,1)S(1)} collective-permute-done((bf16[128,4096]{1,0:T(8,128)(2,1)}, bf16[128,4096]{1,0:T(8,128)(2,1)S(1)}, u32[]{:S(2)}, u32[]{:S(2)}) %collective-permute-start.5) | collective-permute-done | bytes 1048608 | tf_op jit(solution)/shard_map/ppermute | solution.py:171
  195.4 8.2 %shard_map.116 = f32[512,1024]{1,0:T(8,128)S(1)} custom-call(bf16[1,512,4096]{2,1,0:T(8,128)(2,1)} %bitcast.30.a_ref, bf16[1,1024,4096]{2,1,0:T(8,128)(2,1)} %bitcast.173, bf16[1,8,1,4096]{3,2,1,0:T(2,128)(2,1)S(1)} %copy-done.3), custom_call_target="tpu_custom_call" | custom-call | flops 4294967296 | bytes 14680064 | tf_op jit(solution)/shard_map/pallas_call | solution.py:95
  212.2 10.3 %convolution_convert_fusion.1 = bf16[4096,1024]{1,0:T(8,128)(2,1)} fusion(bf16[512,4096]{1,0:T(8,128)(2,1)} %bitcast.24, bf16[512,1024]{0,1:T(8,128)(2,1)} %bitcast.165), kind=kOutput, calls=%fused_computation.5 | convolution fusion | flops 4299161600 | bytes 13631488 | tf_op jit(solution)/shard_map/tm,tf->mf/dot_general | solution.py:326
  237.6 16.3 %while.23 = (s32[]{:T(128)}, f32[8,128,128]{2,1,0:T(8,128)S(1)}, s32[]{:T(128)}, bf16[8,8,128,128]{3,2,1,0:T(8,128)(2,1)}, s32[]{:T(128)}, /*index=5*/s32[]{:T(128)}, s32[]{:T(128)}, s32[]{:T(128)}) while((s32[]{:T(128)}, f32[8,128,128]{2,1,0:T(8,128)S(1)}, s32[]{:T(128)}, bf16[8,8,128,128]{3,2,1,0:T(8,128)(2,1)}, s32[]{:T(128)}, ...), condition=%wide.region_5.6_spmd, body=%wide.region_4.5_spmd.sunk | while | flops 262150 | bytes 1310855 | solution.py:244
  266.5 21.1 %convolution_convert_fusion = bf16[4096,3,1024]{2,0,1:T(8,128)(2,1)} fusion(bf16[512,4096,1]{1,0,2:T(8,128)(2,1)} %bitcast.167, bf16[1,512,1024]{2,1,0:T(8,128)(2,1)S(1)} %copy.125, bf16[1,512,1024]{2,1,0:T(8,128)(2,1)} %copy.124, bf16[1,512,1024]{2,1,0:T(8,128)(2,1)} %copy.123), kind=kOutput, calls=%fused_computation.2 | convolution fusion | flops 12906921984 | bytes 32505856 | tf_op jit(solution)/shard_map/tm,ptc->mpc/dot_general | solution.py:367
  292.0 21.6 %shard_map.117 = bf16[512,4096]{1,0:T(8,128)(2,1)} custom-call(bf16[3,512,1024]{2,1,0:T(8,128)(2,1)S(1)} %pad_maximum_fusion.a_ref, bf16[3,4096,1024]{2,1,0:T(8,128)(2,1)} %bitcast.144, bf16[3,32,1,1024]{3,2,1,0:T(2,128)(2,1)S(1)} %broadcast_in_dim.120.m_ref), custom_call_target="tpu_custom_call" | custom-call | flops 12884901888 | bytes 41943040 | tf_op jit(solution)/shard_map/pallas_call | solution.py:95
  319.8 23.2 %collective-permute-done.9 = bf16[128,4096]{1,0:T(8,128)(2,1)S(1)} collective-permute-done((bf16[128,4096]{1,0:T(8,128)(2,1)S(1)}, bf16[128,4096]{1,0:T(8,128)(2,1)S(1)}, u32[]{:S(2)}, u32[]{:S(2)}) %collective-permute-start.9) | collective-permute-done | bytes 1048608 | tf_op jit(solution)/shard_map/ppermute | solution.py:152
  349.3 7.2 %reshape.106 = f32[512,3,1024]{2,0,1:T(8,128)} reshape(f32[4,128,3,8,128]{4,3,1,0,2:T(8,128)} %broadcast_in_dim.118) | data formatting | bytes 12582912 | tf_op jit(solution)/shard_map/reshape | solution.py:375
  356.5 9.1 %collective-permute-done.7 = bf16[128,4096]{1,0:T(8,128)(2,1)} collective-permute-done((bf16[128,4096]{1,0:T(8,128)(2,1)S(1)}, bf16[128,4096]{1,0:T(8,128)(2,1)}, u32[]{:S(2)}, u32[]{:S(2)}) %collective-permute-start.7) | collective-permute-done | bytes 1048608 | tf_op jit(solution)/shard_map/ppermute | solution.py:205
  368.4 19.7 %collective-permute-done.10 = bf16[128,4096]{1,0:T(8,128)(2,1)} collective-permute-done((bf16[128,4096]{1,0:T(8,128)(2,1)}, bf16[128,4096]{1,0:T(8,128)(2,1)}, u32[]{:S(2)}, u32[]{:S(2)}) %collective-permute-start.10) | collective-permute-done | bytes 1048608 | tf_op jit(solution)/shard_map/ppermute | solution.py:152
  391.1 19.3 %collective-permute-done.8 = bf16[128,4096]{1,0:T(8,128)(2,1)S(1)} collective-permute-done((bf16[128,4096]{1,0:T(8,128)(2,1)}, bf16[128,4096]{1,0:T(8,128)(2,1)S(1)}, u32[]{:S(2)}, u32[]{:S(2)}) %collective-permute-start.8) | collective-permute-done | bytes 1048608 | tf_op jit(solution)/shard_map/ppermute | solution.py:205
  413.1 18.2 %collective-permute-done.11 = bf16[128,4096]{1,0:T(8,128)(2,1)} collective-permute-done((bf16[128,4096]{1,0:T(8,128)(2,1)}, bf16[128,4096]{1,0:T(8,128)(2,1)}, u32[]{:S(2)}, u32[]{:S(2)}) %collective-permute-start.11) | collective-permute-done | bytes 1048608 | tf_op jit(solution)/shard_map/ppermute | solution.py:152
  438.5 34.6 %reduce-scatter.3.cloned.1.call-done = bf16[512,3,1024]{2,0,1:T(8,128)(2,1)} async-done(((bf16[4096,3,1024]{2,0,1:T(8,128)(2,1)}), bf16[512,3,1024]{2,0,1:T(8,128)(2,1)}) %reduce-scatter.3.cloned.1.call-update) | async-done | bytes 3145744 | tf_op jit(solution)/shard_map/reduce_scatter | solution.py:368
  473.1 8.0 %multiply_multiply_fusion = f32[512,3,1024]{2,0,1:T(8,128)} fusion(f32[512,3,1024]{2,0,1:T(8,128)} %reshape.106, bf16[512,3,1024]{2,0,1:T(8,128)(2,1)} %reduce-scatter.3.cloned.1.call-done), kind=kLoop, calls=%fused_computation.6 | loop fusion | flops 4718592 | bytes 15728640 | tf_op jit(solution)/shard_map/mul | solution.py:376
  (164 shorter events, 119.4 us)
Async XLA Ops:
  7.2 137.6 %all-gather.5.cloned.1.call-start = ((), (), s32[]{:S(2)}) async-start(), calls=%async_computation.4 | async-start | bytes 2359296 | tf_op jit(solution)/shard_map/all_gather | solution.py:222
  7.2 28.5 %collective-permute-start = (bf16[128,4096]{1,0:T(8,128)(2,1)}, bf16[128,4096]{1,0:T(8,128)(2,1)S(1)}, u32[]{:S(2)}, u32[]{:S(2)}) collective-permute-start(bf16[128,4096]{1,0:T(8,128)(2,1)} %a_ref.1), channel_id=1, source_target_pairs={{0,1},{1,2},{2,3},{3,0},{4,5},{5,6},{6,7},{7,4},{8,9},{9,10},{10,1... | collective-permute-start | bytes 3145736 | tf_op jit(solution)/shard_map/ppermute | solution.py:132
  14.1 130.7 %copy-start.22 = (bf16[512,8]{0,1:T(8,128)(2,1)}, bf16[512,8]{0,1:T(8,128)(2,1)S(1)}, u32[]{:S(2)}) copy-start(bf16[512,8]{0,1:T(8,128)(2,1)S(1)} %get-tuple-element.134) | copy-start | bytes 24580
  15.5 101.4 %copy-start.25 = (bf16[512,8]{0,1:T(8,128)(2,1)}, bf16[512,8]{0,1:T(8,128)(2,1)S(1)}, u32[]{:S(2)}) copy-start(bf16[512,8]{0,1:T(8,128)(2,1)S(1)} %get-tuple-element.136) | copy-start | bytes 24580
  35.7 26.1 %collective-permute-start.1 = (bf16[128,4096]{1,0:T(8,128)(2,1)S(1)}, bf16[128,4096]{1,0:T(8,128)(2,1)S(1)}, u32[]{:S(2)}, u32[]{:S(2)}) collective-permute-start(bf16[128,4096]{1,0:T(8,128)(2,1)S(1)} %collective-permute-done.a_ref), channel_id=1, source_target_pairs={{0,1},{1,2},{2,3},{3,0},{4,5},{5,6},{6,7},{7,4},{8,9},{9,10},{10,1... | collective-permute-start | bytes 3145736 | tf_op jit(solution)/shard_map/ppermute | solution.py:132
  37.1 38.7 %copy-start.17 = (bf16[4,128,4096]{2,1,0:T(8,128)(2,1)}, bf16[4,128,4096]{2,1,0:T(8,128)(2,1)S(1)}, u32[]{:S(2)}) copy-start(bf16[4,128,4096]{2,1,0:T(8,128)(2,1)S(1)} %bitcast_dynamic-update-slice_fusion.3) | copy-start | bytes 12582916
  61.8 28.2 %collective-permute-start.2 = (bf16[128,4096]{1,0:T(8,128)(2,1)S(1)}, bf16[128,4096]{1,0:T(8,128)(2,1)S(1)}, u32[]{:S(2)}, u32[]{:S(2)}) collective-permute-start(bf16[128,4096]{1,0:T(8,128)(2,1)S(1)} %collective-permute-done.1.a_ref), channel_id=1, source_target_pairs={{0,1},{1,2},{2,3},{3,0},{4,5},{5,6},{6,7},{7,4},{8,9},{9,10},{10,1... | collective-permute-start | bytes 3145736 | tf_op jit(solution)/shard_map/ppermute | solution.py:132
  113.2 124.4 %all-gather.7.cloned.1.call-start = ((), (), s32[]{:S(2)}) async-start(), calls=%async_computation.5 | async-start | bytes 2359296 | tf_op jit(solution)/shard_map/all_gather | solution.py:235
  116.8 28.0 %copy-start.10 = (bf16[1,512,1024]{1,2,0:T(8,128)(2,1)}, bf16[1,512,1024]{1,2,0:T(8,128)(2,1)S(1)}, u32[]{:S(2)}) copy-start(bf16[1,512,1024]{1,2,0:T(8,128)(2,1)S(1)} %copy.121) | copy-start | bytes 3145732
  116.8 25.6 %collective-permute-start.3 = (bf16[128,4096]{1,0:T(8,128)(2,1)}, bf16[128,4096]{1,0:T(8,128)(2,1)}, u32[]{:S(2)}, u32[]{:S(2)}) collective-permute-start(bf16[128,4096]{1,0:T(8,128)(2,1)} %param.19), channel_id=1, source_target_pairs={{0,1},{1,2},{2,3},{3,0},{4,5},{5,6},{6,7},{7,4},{8,9},{9,10},{10,1... | collective-permute-start | bytes 3145736 | tf_op jit(solution)/shard_map/ppermute | solution.py:171
  142.4 24.6 %collective-permute-start.4 = (bf16[128,4096]{1,0:T(8,128)(2,1)}, bf16[128,4096]{1,0:T(8,128)(2,1)}, u32[]{:S(2)}, u32[]{:S(2)}) collective-permute-start(bf16[128,4096]{1,0:T(8,128)(2,1)} %collective-permute-done.3), channel_id=1, source_target_pairs={{0,1},{1,2},{2,3},{3,0},{4,5},{5,6},{6,7},{7,4},{8,9},{9,10},{10,1... | collective-permute-start | bytes 3145736 | tf_op jit(solution)/shard_map/ppermute | solution.py:171
  170.1 23.9 %collective-permute-start.5 = (bf16[128,4096]{1,0:T(8,128)(2,1)}, bf16[128,4096]{1,0:T(8,128)(2,1)S(1)}, u32[]{:S(2)}, u32[]{:S(2)}) collective-permute-start(bf16[128,4096]{1,0:T(8,128)(2,1)} %collective-permute-done.4), channel_id=1, source_target_pairs={{0,1},{1,2},{2,3},{3,0},{4,5},{5,6},{6,7},{7,4},{8,9},{9,10},{10,1... | collective-permute-start | bytes 3145736 | tf_op jit(solution)/shard_map/ppermute | solution.py:171
  212.1 222.2 %reduce-scatter.5.cloned.1.call-start = ((), (), s32[]{:S(2)}) async-start(), calls=%async_computation.3 | async-start | bytes 9437184 | tf_op jit(solution)/shard_map/reduce_scatter | solution.py:327
  222.5 250.6 %reduce-scatter.3.cloned.1.call-start = ((), (), s32[]{:S(2)}) async-start(), calls=%async_computation.2 | async-start | bytes 28311552 | tf_op jit(solution)/shard_map/reduce_scatter | solution.py:368
  290.1 26.7 %collective-permute-start.6 = (bf16[128,4096]{1,0:T(8,128)(2,1)}, bf16[128,4096]{1,0:T(8,128)(2,1)}, u32[]{:S(2)}, u32[]{:S(2)}) collective-permute-start(bf16[128,4096]{1,0:T(8,128)(2,1)} %dynamic-slice_bitcast_fusion.1), channel_id=1, source_target_pairs={{0,1},{1,2},{2,3},{3,0},{4,5},{5,6},{6,7},{7,4},{8,9},{9,10},{10,1... | collective-permute-start | bytes 3145736 | tf_op jit(solution)/shard_map/ppermute | solution.py:205
  314.8 28.2 %collective-permute-start.9 = (bf16[128,4096]{1,0:T(8,128)(2,1)S(1)}, bf16[128,4096]{1,0:T(8,128)(2,1)S(1)}, u32[]{:S(2)}, u32[]{:S(2)}) collective-permute-start(bf16[128,4096]{1,0:T(8,128)(2,1)S(1)} %dynamic-slice_bitcast_fusion), channel_id=1, source_target_pairs={{0,1},{1,2},{2,3},{3,0},{4,5},{5,6},{6,7},{7,4},{8,9},{9,10},{10,1... | collective-permute-start | bytes 3145736 | tf_op jit(solution)/shard_map/ppermute | solution.py:152
  316.5 29.2 %copy-start.29 = (s32[3,32,8]{1,2,0:T(8,128)S(1)}, s32[3,32,8]{1,2,0:T(8,128)}, u32[]{:S(2)}) copy-start(s32[3,32,8]{1,2,0:T(8,128)} %param.16) | copy-start | bytes 9220
  318.6 47.0 %collective-permute-start.7 = (bf16[128,4096]{1,0:T(8,128)(2,1)S(1)}, bf16[128,4096]{1,0:T(8,128)(2,1)}, u32[]{:S(2)}, u32[]{:S(2)}) collective-permute-start(bf16[128,4096]{1,0:T(8,128)(2,1)S(1)} %fusion.9), channel_id=1, source_target_pairs={{0,1},{1,2},{2,3},{3,0},{4,5},{5,6},{6,7},{7,4},{8,9},{9,10},{10,1... | collective-permute-start | bytes 3145736 | tf_op jit(solution)/shard_map/ppermute | solution.py:205
  345.6 42.4 %collective-permute-start.10 = (bf16[128,4096]{1,0:T(8,128)(2,1)}, bf16[128,4096]{1,0:T(8,128)(2,1)}, u32[]{:S(2)}, u32[]{:S(2)}) collective-permute-start(bf16[128,4096]{1,0:T(8,128)(2,1)} %fusion.5), channel_id=1, source_target_pairs={{0,1},{1,2},{2,3},{3,0},{4,5},{5,6},{6,7},{7,4},{8,9},{9,10},{10,1... | collective-permute-start | bytes 3145736 | tf_op jit(solution)/shard_map/ppermute | solution.py:152
  356.5 34.4 %copy-start.30 = (s32[8,32]{1,0:T(8,128)S(1)}, s32[8,32]{1,0:T(8,128)}, u32[]{:S(2)}) copy-start(s32[8,32]{1,0:T(8,128)} %param.18) | copy-start | bytes 3076
  356.5 53.9 %copy-start.1 = (bf16[128,4096]{1,0:T(8,128)(2,1)S(1)}, bf16[128,4096]{1,0:T(8,128)(2,1)}, u32[]{:S(2)}) copy-start(bf16[128,4096]{1,0:T(8,128)(2,1)} %a_ref.1) | copy-start | bytes 3145732
  368.4 63.0 %copy-start.16 = (bf16[128,4096]{1,0:T(8,128)(2,1)S(1)}, bf16[128,4096]{1,0:T(8,128)(2,1)}, u32[]{:S(2)}) copy-start(bf16[128,4096]{1,0:T(8,128)(2,1)} %param.19) | copy-start | bytes 3145732
  368.4 42.1 %collective-permute-start.8 = (bf16[128,4096]{1,0:T(8,128)(2,1)}, bf16[128,4096]{1,0:T(8,128)(2,1)S(1)}, u32[]{:S(2)}, u32[]{:S(2)}) collective-permute-start(bf16[128,4096]{1,0:T(8,128)(2,1)} %fusion.8), channel_id=1, source_target_pairs={{0,1},{1,2},{2,3},{3,0},{4,5},{5,6},{6,7},{7,4},{8,9},{9,10},{10,1... | collective-permute-start | bytes 3145736 | tf_op jit(solution)/shard_map/ppermute | solution.py:205
  390.9 40.4 %collective-permute-start.11 = (bf16[128,4096]{1,0:T(8,128)(2,1)}, bf16[128,4096]{1,0:T(8,128)(2,1)}, u32[]{:S(2)}, u32[]{:S(2)}) collective-permute-start(bf16[128,4096]{1,0:T(8,128)(2,1)} %fusion.4), channel_id=1, source_target_pairs={{0,1},{1,2},{2,3},{3,0},{4,5},{5,6},{6,7},{7,4},{8,9},{9,10},{10,1... | collective-permute-start | bytes 3145736 | tf_op jit(solution)/shard_map/ppermute | solution.py:152
  (23 other events, 127.8 us)
Sparse Core Ops, SparseCore 0:
  113.3 29.1 all-gather.4
  212.2 25.2 all-gather.6
  241.0 71.2 reduce-scatter.4
  316.2 156.8 reduce-scatter.2

commit v2 on v1

--- a/solution.py
+++ b/solution.py
@@ -364,10 +364,13 @@
         ],
         axis=0,
     ).reshape(3, block_rows, features)
-    qkv_part = jnp.einsum("tm,ptc->mpc", gathered, grad_proj, preferred_element_type=jnp.float32)
-    qkv_sum = lax.psum_scatter(
-        qkv_part.astype(jnp.bfloat16), "ctx", scatter_dimension=0, tiled=True
-    ).astype(jnp.float32)
+    plane_sums = {}
+    for plane in (2, 1, 0):
+        plane_part = jnp.dot(
+            gathered.T, grad_proj[plane], preferred_element_type=jnp.float32
+        ).astype(jnp.bfloat16)
+        plane_sums[plane] = lax.psum_scatter(plane_part, "ctx", scatter_dimension=0, tiled=True)
+    qkv_sum = jnp.stack([plane_sums[plane] for plane in range(3)], axis=1).astype(jnp.float32)
     qkv_keep = lax.dynamic_slice_in_dim(qkv_blocks, ctx_place * slice_blocks, slice_blocks, 1)
     qkv_keep = jnp.broadcast_to(
         jnp.transpose(qkv_keep, (1, 0, 2)).astype(jnp.float32)[:, None, :, :, None],

time: 498 us -> 556 us (1.12)
  waiting for transfers between devices: 202 us -> 270 us
  loops' own time: 8.81 us -> 0.18 us
  matrix products: 66.5 us -> 60.5 us
  local copies, waits for them, and re-layouts: 51.3 us -> 56.9 us
    reduce_scatter x1 -> x3, waiting for transfers between devices: 34.6 us -> 110 us  [on_device(): lax.psum_scatter(plane_part, 'ctx', scatter_dimension=0, tiled=True)]
    another operation x1, loops' own time: 8.79 us -> 0.17 us  [entering(): return lax.fori_loop(0, ahead, entering_one, state)]
    ppermute x3, waiting for transfers between devices: 47.5 us -> 41.9 us  [advance(): moved = lax.ppermute(self.moving, self.axis, self.step)]
    dot_general x1 -> x3, matrix products: 21.1 us -> 21.1 us  [on_device(): jnp.dot(gathered.T, grad_proj[plane], preferred_element_type=jnp.float32)]
  transfers between devices with their start and end apart: 16 -> 18, of which waited for: 13 -> 13; matrix products, arithmetic and copies ran while one was open for 27% -> 23% of each run, Pallas kernels for 15% -> 13%
where the time goes in v2:
time: 556 us; the launch traced here: 547 us
  waiting for transfers between devices  270 us (49%)
  Pallas kernels  93.1 us (17%)
  matrix products  60.5 us (11%)
  local copies, waits for them, and re-layouts  56.9 us (10%)
  other arithmetic  43.1 us (8%)
  between operations  15.2 us (3%)
  starting transfers between devices  7.77 us (1%)
    reduce_scatter x3, waiting for transfers between devices, on_device(): lax.psum_scatter(plane_part, 'ctx', scatter_dimension=0, tiled=True)  110 us
    pallas_call x5, Pallas kernels, masked_matmul_nn(): pl.pallas_call(_nn_kernel, grid=grid, in_specs=[pl.BlockSpec((m, tk), lam...  63.2 us
    ppermute x3, waiting for transfers between devices, ring_scatter(): arrived = lax.ppermute(running.astype(jnp.bfloat16), axis, step)  59.6 us
    ppermute x3, waiting for transfers between devices, advance(): moved = lax.ppermute(self.moving, self.axis, self.step)  41.9 us
    pallas_call x2, Pallas kernels, masked_matmul_nt(): pl.pallas_call(_nt_kernel, grid=grid, in_specs=[pl.BlockSpec((None, m, tk...  29.9 us
    ppermute x3, waiting for transfers between devices, ring_gather(): moving = lax.ppermute(moving, axis, step)  29.2 us
    ppermute x3, waiting for transfers between devices, advance(): lax.ppermute(self.running.astype(jnp.bfloat16), self.axis, self.step)  28.9 us
    dot_general x3, matrix products, on_device(): jnp.dot(gathered.T, grad_proj[plane], preferred_element_type=jnp.float32)  21.1 us
  transfers between devices with their start and end apart: 18, of which 13 were waited for; matrix products, arithmetic and copies ran while one was open for 23% of the time, Pallas kernels for 13%

profile of v2, /device:TPU:0, one launch (start us, length us, event | category | flops | bytes accessed | tf_op | source)
XLA Modules:
  0.0 546.7 jit_solution(2182994601004135527)
XLA Ops:
  16.7 14.0 %shard_map.111 = bf16[3,128,1024]{2,1,0:T(8,128)(2,1)S(1)} custom-call(bf16[128,4096]{1,0:T(8,128)(2,1)S(1)} %copy-done, bf16[3,4096,1024]{2,1,0:T(8,128)(2,1)} %bitcast.149, bf16[3,32,1,1024]{3,2,1,0:T(2,128)(2,1)S(1)} %broadcast_in_dim.120.m_ref), custom_call_target="tpu_custom_call" | custom-call | flops 3221225472 | bytes 29097984 | tf_op jit(solution)/shard_map/pallas_call | solution.py:66
  37.1 24.7 %collective-permute-done.1.a_ref = bf16[128,4096]{1,0:T(8,128)(2,1)S(1)} collective-permute-done((bf16[128,4096]{1,0:T(8,128)(2,1)S(1)}, bf16[128,4096]{1,0:T(8,128)(2,1)S(1)}, u32[]{:S(2)}, u32[]{:S(2)}) %collective-permute-start.1) | collective-permute-done | bytes 1048608 | tf_op jit(solution)/shard_map/ppermute | solution.py:132
  61.8 14.0 %shard_map.112 = bf16[3,128,1024]{2,1,0:T(8,128)(2,1)S(1)} custom-call(bf16[128,4096]{1,0:T(8,128)(2,1)S(1)} %collective-permute-done.a_ref, bf16[3,4096,1024]{2,1,0:T(8,128)(2,1)} %bitcast.150, bf16[3,32,1,1024]{3,2,1,0:T(2,128)(2,1)S(1)} %broadcast_in_dim.120.m_ref), custom_call_target="tpu_custom_call" | custom-call | flops 3221225472 | bytes 29097984 | tf_op jit(solution)/shard_map/pallas_call | solution.py:66
  75.9 14.0 %shard_map.113 = bf16[3,128,1024]{2,1,0:T(8,128)(2,1)S(1)} custom-call(bf16[128,4096]{1,0:T(8,128)(2,1)S(1)} %collective-permute-done.1.a_ref, bf16[3,4096,1024]{2,1,0:T(8,128)(2,1)} %bitcast.151, bf16[3,32,1,1024]{3,2,1,0:T(2,128)(2,1)S(1)} %broadcast_in_dim.120.m_ref), custom_call_target="tpu_custom_call" | custom-call | flops 3221225472 | bytes 29097984 | tf_op jit(solution)/shard_map/pallas_call | solution.py:66
  90.0 14.0 %shard_map.114 = bf16[3,128,1024]{2,1,0:T(8,128)(2,1)S(1)} custom-call(bf16[128,4096]{1,0:T(8,128)(2,1)S(1)} %collective-permute-done.2.a_ref, bf16[3,4096,1024]{2,1,0:T(8,128)(2,1)} %bitcast.152, bf16[3,32,1,1024]{3,2,1,0:T(2,128)(2,1)S(1)} %broadcast_in_dim.120.m_ref), custom_call_target="tpu_custom_call" | custom-call | flops 3221225472 | bytes 29097984 | tf_op jit(solution)/shard_map/pallas_call | solution.py:66
  126.3 14.6 %collective-permute-done.3 = bf16[128,4096]{1,0:T(8,128)(2,1)} collective-permute-done((bf16[128,4096]{1,0:T(8,128)(2,1)}, bf16[128,4096]{1,0:T(8,128)(2,1)}, u32[]{:S(2)}, u32[]{:S(2)}) %collective-permute-start.3) | collective-permute-done | bytes 1048608 | tf_op jit(solution)/shard_map/ppermute | solution.py:171
  148.4 17.1 %collective-permute-done.4 = bf16[128,4096]{1,0:T(8,128)(2,1)} collective-permute-done((bf16[128,4096]{1,0:T(8,128)(2,1)}, bf16[128,4096]{1,0:T(8,128)(2,1)}, u32[]{:S(2)}, u32[]{:S(2)}) %collective-permute-start.4) | collective-permute-done | bytes 1048608 | tf_op jit(solution)/shard_map/ppermute | solution.py:171
  168.7 7.2 %shard_map.115 = bf16[1,512,4096]{2,1,0:T(8,128)(2,1)S(1)} custom-call(bf16[512,1024]{1,0:T(8,128)(2,1)S(1)} %copy.119.a_ref, bf16[1,1024,4096]{2,1,0:T(8,128)(2,1)} %bitcast.189, bf16[1,8,1,4096]{3,2,1,0:T(2,128)(2,1)S(1)} %copy-done.3), custom_call_target="tpu_custom_call" | custom-call | flops 4294967296 | bytes 16777216 | tf_op jit(solution)/shard_map/pallas_call | solution.py:66
  179.1 10.2 %collective-permute-done.5 = bf16[128,4096]{1,0:T(8,128)(2,1)} collective-permute-done((bf16[128,4096]{1,0:T(8,128)(2,1)}, bf16[128,4096]{1,0:T(8,128)(2,1)}, u32[]{:S(2)}, u32[]{:S(2)}) %collective-permute-start.5) | collective-permute-done | bytes 1048608 | tf_op jit(solution)/shard_map/ppermute | solution.py:171
  192.0 8.2 %shard_map.116 = f32[512,1024]{1,0:T(8,128)S(1)} custom-call(bf16[1,512,4096]{2,1,0:T(8,128)(2,1)} %bitcast.30.a_ref, bf16[1,1024,4096]{2,1,0:T(8,128)(2,1)} %bitcast.190, bf16[1,8,1,4096]{3,2,1,0:T(2,128)(2,1)S(1)} %copy-done.3), custom_call_target="tpu_custom_call" | custom-call | flops 4294967296 | bytes 14680064 | tf_op jit(solution)/shard_map/pallas_call | solution.py:95
  208.7 9.2 %convolution_convert_fusion = bf16[4096,1024]{1,0:T(8,128)(2,1)} fusion(bf16[512,4096]{1,0:T(8,128)(2,1)} %bitcast.24, bf16[512,1024]{0,1:T(8,128)(2,1)S(1)} %bitcast.174), kind=kOutput, calls=%fused_computation.4 | convolution fusion | flops 4299161600 | bytes 13631488 | tf_op jit(solution)/shard_map/tm,tf->mf/dot_general | solution.py:326
  226.5 7.0 %convolution_convert_fusion.3 = bf16[4096,1024]{1,0:T(8,128)(2,1)} fusion(bf16[512,4096]{1,0:T(8,128)(2,1)S(1)} %bitcast.177, bf16[512,1024]{0,1:T(8,128)(2,1)S(1)} %bitcast.180), kind=kOutput, calls=%fused_computation.7 | convolution fusion | flops 4299161600 | bytes 13631488 | tf_op jit(solution)/shard_map/dot_general | solution.py:369
  233.9 7.7 %while.23 = (s32[]{:T(128)}, f32[8,128,128]{2,1,0:T(8,128)S(1)}, s32[]{:T(128)}, bf16[8,8,128,128]{3,2,1,0:T(8,128)(2,1)}, s32[]{:T(128)}, /*index=5*/s32[]{:T(128)}, s32[]{:T(128)}, s32[]{:T(128)}) while((s32[]{:T(128)}, f32[8,128,128]{2,1,0:T(8,128)S(1)}, s32[]{:T(128)}, bf16[8,8,128,128]{3,2,1,0:T(8,128)(2,1)}, s32[]{:T(128)}, ...), condition=%wide.region_5.6_spmd, body=%wide.region_4.5_spmd.sunk | while | flops 262150 | bytes 1310863 | solution.py:244
  249.2 7.1 %convolution_convert_fusion.1 = bf16[4096,1024]{1,0:T(8,128)(2,1)} fusion(bf16[512,4096]{1,0:T(8,128)(2,1)S(1)} %bitcast.178, bf16[512,1024]{0,1:T(8,128)(2,1)S(1)} %bitcast.175), kind=kOutput, calls=%fused_computation.5 | convolution fusion | flops 4299161600 | bytes 13631488 | tf_op jit(solution)/shard_map/dot_general | solution.py:369
  263.0 7.1 %convolution_convert_fusion.2 = bf16[4096,1024]{1,0:T(8,128)(2,1)} fusion(bf16[512,4096]{1,0:T(8,128)(2,1)S(1)} %bitcast.179, bf16[512,1024]{0,1:T(8,128)(2,1)S(1)} %bitcast.182), kind=kOutput, calls=%fused_computation.6 | convolution fusion | flops 4299161600 | bytes 13631488 | tf_op jit(solution)/shard_map/dot_general | solution.py:369
  278.4 21.7 %shard_map.117 = bf16[512,4096]{1,0:T(8,128)(2,1)} custom-call(bf16[3,512,1024]{2,1,0:T(8,128)(2,1)S(1)} %pad_maximum_fusion.a_ref, bf16[3,4096,1024]{2,1,0:T(8,128)(2,1)} %bitcast.153, bf16[3,32,1,1024]{3,2,1,0:T(2,128)(2,1)S(1)} %broadcast_in_dim.120.m_ref), custom_call_target="tpu_custom_call" | custom-call | flops 12884901888 | bytes 41943040 | tf_op jit(solution)/shard_map/pallas_call | solution.py:95
  306.1 23.2 %collective-permute-done.9 = bf16[128,4096]{1,0:T(8,128)(2,1)S(1)} collective-permute-done((bf16[128,4096]{1,0:T(8,128)(2,1)S(1)}, bf16[128,4096]{1,0:T(8,128)(2,1)S(1)}, u32[]{:S(2)}, u32[]{:S(2)}) %collective-permute-start.9) | collective-permute-done | bytes 1048608 | tf_op jit(solution)/shard_map/ppermute | solution.py:152
  335.2 7.2 %reshape.115 = f32[512,3,1024]{2,0,1:T(8,128)} reshape(f32[4,128,3,8,128]{4,3,1,0,2:T(8,128)} %broadcast_in_dim.118) | data formatting | bytes 12582912 | tf_op jit(solution)/shard_map/reshape | solution.py:378
  342.4 9.6 %collective-permute-done.7 = bf16[128,4096]{1,0:T(8,128)(2,1)} collective-permute-done((bf16[128,4096]{1,0:T(8,128)(2,1)S(1)}, bf16[128,4096]{1,0:T(8,128)(2,1)}, u32[]{:S(2)}, u32[]{:S(2)}) %collective-permute-start.7) | collective-permute-done | bytes 1048608 | tf_op jit(solution)/shard_map/ppermute | solution.py:205
  354.9 19.5 %collective-permute-done.10 = bf16[128,4096]{1,0:T(8,128)(2,1)} collective-permute-done((bf16[128,4096]{1,0:T(8,128)(2,1)}, bf16[128,4096]{1,0:T(8,128)(2,1)}, u32[]{:S(2)}, u32[]{:S(2)}) %collective-permute-start.10) | collective-permute-done | bytes 1048608 | tf_op jit(solution)/shard_map/ppermute | solution.py:152
  377.4 19.4 %collective-permute-done.8 = bf16[128,4096]{1,0:T(8,128)(2,1)S(1)} collective-permute-done((bf16[128,4096]{1,0:T(8,128)(2,1)}, bf16[128,4096]{1,0:T(8,128)(2,1)S(1)}, u32[]{:S(2)}, u32[]{:S(2)}) %collective-permute-start.8) | collective-permute-done | bytes 1048608 | tf_op jit(solution)/shard_map/ppermute | solution.py:205
  399.6 16.8 %collective-permute-done.11 = bf16[128,4096]{1,0:T(8,128)(2,1)S(1)} collective-permute-done((bf16[128,4096]{1,0:T(8,128)(2,1)}, bf16[128,4096]{1,0:T(8,128)(2,1)S(1)}, u32[]{:S(2)}, u32[]{:S(2)}) %collective-permute-start.11) | collective-permute-done | bytes 1048608 | tf_op jit(solution)/shard_map/ppermute | solution.py:152
  423.3 35.0 %reduce-scatter.9.cloned.1.call-done = bf16[512,1024]{1,0:T(8,128)(2,1)} async-done(((bf16[4096,1024]{1,0:T(8,128)(2,1)}), bf16[512,1024]{1,0:T(8,128)(2,1)}) %reduce-scatter.9.cloned.1.call-update) | async-done | bytes 1048592 | tf_op jit(solution)/shard_map/reduce_scatter | solution.py:372
  458.3 75.0 %reduce-scatter.7.cloned.1.call-done = bf16[512,1024]{1,0:T(8,128)(2,1)} async-done(((bf16[4096,1024]{1,0:T(8,128)(2,1)}), bf16[512,1024]{1,0:T(8,128)(2,1)}) %reduce-scatter.7.cloned.1.call-update) | async-done | bytes 1048592 | tf_op jit(solution)/shard_map/reduce_scatter | solution.py:372
  (188 shorter events, 135.8 us)
Async XLA Ops:
  7.2 136.0 %all-gather.5.cloned.1.call-start = ((), (), s32[]{:S(2)}) async-start(), calls=%async_computation.8 | async-start | bytes 2359296 | tf_op jit(solution)/shard_map/all_gather | solution.py:222
  7.2 28.5 %collective-permute-start = (bf16[128,4096]{1,0:T(8,128)(2,1)}, bf16[128,4096]{1,0:T(8,128)(2,1)S(1)}, u32[]{:S(2)}, u32[]{:S(2)}) collective-permute-start(bf16[128,4096]{1,0:T(8,128)(2,1)} %a_ref.1), channel_id=1, source_target_pairs={{0,1},{1,2},{2,3},{3,0},{4,5},{5,6},{6,7},{7,4},{8,9},{9,10},{10,1... | collective-permute-start | bytes 3145736 | tf_op jit(solution)/shard_map/ppermute | solution.py:132
  14.2 102.6 %copy-start.33 = (bf16[512,8]{0,1:T(8,128)(2,1)}, bf16[512,8]{0,1:T(8,128)(2,1)S(1)}, u32[]{:S(2)}) copy-start(bf16[512,8]{0,1:T(8,128)(2,1)S(1)} %get-tuple-element.136) | copy-start | bytes 24580
  15.5 127.7 %copy-start.30 = (bf16[512,8]{0,1:T(8,128)(2,1)}, bf16[512,8]{0,1:T(8,128)(2,1)S(1)}, u32[]{:S(2)}) copy-start(bf16[512,8]{0,1:T(8,128)(2,1)S(1)} %get-tuple-element.134) | copy-start | bytes 24580
  35.7 26.1 %collective-permute-start.1 = (bf16[128,4096]{1,0:T(8,128)(2,1)S(1)}, bf16[128,4096]{1,0:T(8,128)(2,1)S(1)}, u32[]{:S(2)}, u32[]{:S(2)}) collective-permute-start(bf16[128,4096]{1,0:T(8,128)(2,1)S(1)} %collective-permute-done.a_ref), channel_id=1, source_target_pairs={{0,1},{1,2},{2,3},{3,0},{4,5},{5,6},{6,7},{7,4},{8,9},{9,10},{10,1... | collective-permute-start | bytes 3145736 | tf_op jit(solution)/shard_map/ppermute | solution.py:132
  37.1 38.7 %copy-start.21 = (bf16[4,128,4096]{2,1,0:T(8,128)(2,1)}, bf16[4,128,4096]{2,1,0:T(8,128)(2,1)S(1)}, u32[]{:S(2)}) copy-start(bf16[4,128,4096]{2,1,0:T(8,128)(2,1)S(1)} %bitcast_dynamic-update-slice_fusion.3) | copy-start | bytes 12582916
  61.8 28.2 %collective-permute-start.2 = (bf16[128,4096]{1,0:T(8,128)(2,1)S(1)}, bf16[128,4096]{1,0:T(8,128)(2,1)S(1)}, u32[]{:S(2)}, u32[]{:S(2)}) collective-permute-start(bf16[128,4096]{1,0:T(8,128)(2,1)S(1)} %collective-permute-done.1.a_ref), channel_id=1, source_target_pairs={{0,1},{1,2},{2,3},{3,0},{4,5},{5,6},{6,7},{7,4},{8,9},{9,10},{10,1... | collective-permute-start | bytes 3145736 | tf_op jit(solution)/shard_map/ppermute | solution.py:132
  113.1 120.8 %all-gather.7.cloned.1.call-start = ((), (), s32[]{:S(2)}) async-start(), calls=%async_computation.9 | async-start | bytes 2359296 | tf_op jit(solution)/shard_map/all_gather | solution.py:235
  115.3 25.5 %collective-permute-start.3 = (bf16[128,4096]{1,0:T(8,128)(2,1)}, bf16[128,4096]{1,0:T(8,128)(2,1)}, u32[]{:S(2)}, u32[]{:S(2)}) collective-permute-start(bf16[128,4096]{1,0:T(8,128)(2,1)} %param.19), channel_id=1, source_target_pairs={{0,1},{1,2},{2,3},{3,0},{4,5},{5,6},{6,7},{7,4},{8,9},{9,10},{10,1... | collective-permute-start | bytes 3145736 | tf_op jit(solution)/shard_map/ppermute | solution.py:171
  140.8 24.6 %collective-permute-start.4 = (bf16[128,4096]{1,0:T(8,128)(2,1)}, bf16[128,4096]{1,0:T(8,128)(2,1)}, u32[]{:S(2)}, u32[]{:S(2)}) collective-permute-start(bf16[128,4096]{1,0:T(8,128)(2,1)} %collective-permute-done.3), channel_id=1, source_target_pairs={{0,1},{1,2},{2,3},{3,0},{4,5},{5,6},{6,7},{7,4},{8,9},{9,10},{10,1... | collective-permute-start | bytes 3145736 | tf_op jit(solution)/shard_map/ppermute | solution.py:171
  165.4 23.9 %collective-permute-start.5 = (bf16[128,4096]{1,0:T(8,128)(2,1)}, bf16[128,4096]{1,0:T(8,128)(2,1)}, u32[]{:S(2)}, u32[]{:S(2)}) collective-permute-start(bf16[128,4096]{1,0:T(8,128)(2,1)} %collective-permute-done.4), channel_id=1, source_target_pairs={{0,1},{1,2},{2,3},{3,0},{4,5},{5,6},{6,7},{7,4},{8,9},{9,10},{10,1... | collective-permute-start | bytes 3145736 | tf_op jit(solution)/shard_map/ppermute | solution.py:171
  208.7 210.7 %reduce-scatter.11.cloned.1.call-start = ((), (), s32[]{:S(2)}) async-start(), calls=%async_computation.7 | async-start | bytes 9437184 | tf_op jit(solution)/shard_map/reduce_scatter | solution.py:327
  218.0 205.4 %reduce-scatter.5.cloned.1.call-start = ((), (), s32[]{:S(2)}) async-start(), calls=%async_computation.4 | async-start | bytes 9437184 | tf_op jit(solution)/shard_map/reduce_scatter | solution.py:372
  233.5 224.8 %reduce-scatter.9.cloned.1.call-start = ((), (), s32[]{:S(2)}) async-start(), calls=%async_computation.6 | async-start | bytes 9437184 | tf_op jit(solution)/shard_map/reduce_scatter | solution.py:372
  256.3 277.1 %reduce-scatter.7.cloned.1.call-start = ((), (), s32[]{:S(2)}) async-start(), calls=%async_computation.5 | async-start | bytes 9437184 | tf_op jit(solution)/shard_map/reduce_scatter | solution.py:372
  272.6 30.2 %collective-permute-start.6 = (bf16[128,4096]{1,0:T(8,128)(2,1)}, bf16[128,4096]{1,0:T(8,128)(2,1)}, u32[]{:S(2)}, u32[]{:S(2)}) collective-permute-start(bf16[128,4096]{1,0:T(8,128)(2,1)} %dynamic-slice_bitcast_fusion.1), channel_id=1, source_target_pairs={{0,1},{1,2},{2,3},{3,0},{4,5},{5,6},{6,7},{7,4},{8,9},{9,10},{10,1... | collective-permute-start | bytes 3145736 | tf_op jit(solution)/shard_map/ppermute | solution.py:205
  301.4 27.9 %collective-permute-start.9 = (bf16[128,4096]{1,0:T(8,128)(2,1)S(1)}, bf16[128,4096]{1,0:T(8,128)(2,1)S(1)}, u32[]{:S(2)}, u32[]{:S(2)}) collective-permute-start(bf16[128,4096]{1,0:T(8,128)(2,1)S(1)} %dynamic-slice_bitcast_fusion), channel_id=1, source_target_pairs={{0,1},{1,2},{2,3},{3,0},{4,5},{5,6},{6,7},{7,4},{8,9},{9,10},{10,1... | collective-permute-start | bytes 3145736 | tf_op jit(solution)/shard_map/ppermute | solution.py:152
  302.8 29.1 %copy-start.37 = (s32[3,32,8]{1,2,0:T(8,128)S(1)}, s32[3,32,8]{1,2,0:T(8,128)}, u32[]{:S(2)}) copy-start(s32[3,32,8]{1,2,0:T(8,128)} %param.16) | copy-start | bytes 9220
  304.6 47.3 %collective-permute-start.7 = (bf16[128,4096]{1,0:T(8,128)(2,1)S(1)}, bf16[128,4096]{1,0:T(8,128)(2,1)}, u32[]{:S(2)}, u32[]{:S(2)}) collective-permute-start(bf16[128,4096]{1,0:T(8,128)(2,1)S(1)} %fusion.9), channel_id=1, source_target_pairs={{0,1},{1,2},{2,3},{3,0},{4,5},{5,6},{6,7},{7,4},{8,9},{9,10},{10,1... | collective-permute-start | bytes 3145736 | tf_op jit(solution)/shard_map/ppermute | solution.py:205
  331.8 42.6 %collective-permute-start.10 = (bf16[128,4096]{1,0:T(8,128)(2,1)}, bf16[128,4096]{1,0:T(8,128)(2,1)}, u32[]{:S(2)}, u32[]{:S(2)}) collective-permute-start(bf16[128,4096]{1,0:T(8,128)(2,1)} %fusion.5), channel_id=1, source_target_pairs={{0,1},{1,2},{2,3},{3,0},{4,5},{5,6},{6,7},{7,4},{8,9},{9,10},{10,1... | collective-permute-start | bytes 3145736 | tf_op jit(solution)/shard_map/ppermute | solution.py:152
  342.4 34.9 %copy-start.38 = (s32[8,32]{1,0:T(8,128)S(1)}, s32[8,32]{1,0:T(8,128)}, u32[]{:S(2)}) copy-start(s32[8,32]{1,0:T(8,128)} %param.18) | copy-start | bytes 3076
  342.4 54.4 %copy-start.1 = (bf16[128,4096]{1,0:T(8,128)(2,1)S(1)}, bf16[128,4096]{1,0:T(8,128)(2,1)}, u32[]{:S(2)}) copy-start(bf16[128,4096]{1,0:T(8,128)(2,1)} %a_ref.1) | copy-start | bytes 3145732
  354.9 41.9 %collective-permute-start.8 = (bf16[128,4096]{1,0:T(8,128)(2,1)}, bf16[128,4096]{1,0:T(8,128)(2,1)S(1)}, u32[]{:S(2)}, u32[]{:S(2)}) collective-permute-start(bf16[128,4096]{1,0:T(8,128)(2,1)} %fusion.8), channel_id=1, source_target_pairs={{0,1},{1,2},{2,3},{3,0},{4,5},{5,6},{6,7},{7,4},{8,9},{9,10},{10,1... | collective-permute-start | bytes 3145736 | tf_op jit(solution)/shard_map/ppermute | solution.py:205
  377.2 39.2 %collective-permute-start.11 = (bf16[128,4096]{1,0:T(8,128)(2,1)}, bf16[128,4096]{1,0:T(8,128)(2,1)S(1)}, u32[]{:S(2)}, u32[]{:S(2)}) collective-permute-start(bf16[128,4096]{1,0:T(8,128)(2,1)} %fusion.4), channel_id=1, source_target_pairs={{0,1},{1,2},{2,3},{3,0},{4,5},{5,6},{6,7},{7,4},{8,9},{9,10},{10,1... | collective-permute-start | bytes 3145736 | tf_op jit(solution)/shard_map/ppermute | solution.py:152
  (33 other events, 139.3 us)
Sparse Core Ops, SparseCore 0:
  113.2 29.1 all-gather.4
  208.8 25.0 all-gather.6
  237.4 71.2 reduce-scatter.10
  312.4 71.2 reduce-scatter.4
  387.0 71.2 reduce-scatter.8
  462.0 71.2 reduce-scatter.6

commit v3 on v0

--- a/solution.py
+++ b/solution.py
@@ -287,7 +287,7 @@
     )
     gathered = gathered.reshape(block_rows, model_width)
     projected = projected.reshape(3, block_rows, features)
-    projected, cotangent_late = lax.optimization_barrier((projected, cotangent))
+    gathered, cotangent_late = lax.optimization_barrier((gathered, cotangent))
     projected = projected.reshape(3, block_rows, local_heads, head_width)
     query_spikes = spike_query.astype(jnp.bfloat16)[:, :, None]
     key_spikes = spike_key.astype(jnp.bfloat16)[:, :, None]

time: 498 us -> 511 us (1.026)
  local copies, waits for them, and re-layouts: 49.9 us -> 67 us
  waiting for transfers between devices: 220 us -> 206 us
  other arithmetic: 42.6 us -> 49 us
    unnamed x73 -> x86, local copies, waits for them, and re-layouts: 4.68 us -> 14.3 us
    reduce_scatter x1, waiting for transfers between devices: 36.5 us -> 27 us  [on_device(): lax.psum_scatter(qkv_part.astype(jnp.bfloat16), 'ctx', scatter_dimension=...]
    reshape x0 -> x1, local copies, waits for them, and re-layouts: none -> 6.59 us  [on_device(): gathered = gathered.reshape(block_rows, model_width)]
    add x7, other arithmetic: 7.73 us -> 14.1 us  [add_states(): return earlier + following]
  transfers between devices with their start and end apart: 16 -> 16, of which waited for: 12 -> 12; matrix products, arithmetic and copies ran while one was open for 25% -> 28% of each run, Pallas kernels for 15% -> 15%
where the time goes in v3:
time: 511 us; the launch traced here: 502 us
  waiting for transfers between devices  206 us (40%)
  Pallas kernels  96.7 us (19%)
  local copies, waits for them, and re-layouts  67 us (13%)
  matrix products  63.7 us (12%)
  other arithmetic  49 us (10%)
  between operations  15 us (3%)
    pallas_call x5, Pallas kernels, masked_matmul_nn(): pl.pallas_call(_nn_kernel, grid=grid, in_specs=[pl.BlockSpec((m, tk), lam...  63.6 us
    ppermute x3, waiting for transfers between devices, ring_scatter(): arrived = lax.ppermute(running.astype(jnp.bfloat16), axis, step)  56.5 us
    ppermute x3, waiting for transfers between devices, advance(): lax.ppermute(self.running.astype(jnp.bfloat16), self.axis, self.step)  46.4 us
    ppermute x3, waiting for transfers between devices, advance(): moved = lax.ppermute(self.moving, self.axis, self.step)  46.4 us
    pallas_call x2, Pallas kernels, masked_matmul_nt(): pl.pallas_call(_nt_kernel, grid=grid, in_specs=[pl.BlockSpec((None, m, tk...  33.1 us
    ppermute x3, waiting for transfers between devices, ring_gather(): moving = lax.ppermute(moving, axis, step)  29.4 us
    reduce_scatter x1, waiting for transfers between devices, on_device(): lax.psum_scatter(qkv_part.astype(jnp.bfloat16), 'ctx', scatter_dimension=...  27 us
    dot_general x1, matrix products, on_device(): jnp.einsum('tm,ptc->mpc', gathered, grad_proj, preferred_element_type=jnp...  21 us
  transfers between devices with their start and end apart: 16, of which 12 were waited for; matrix products, arithmetic and copies ran while one was open for 28% of the time, Pallas kernels for 15%

profile of v3, /device:TPU:0, one launch (start us, length us, event | category | flops | bytes accessed | tf_op | source)
XLA Modules:
  0.0 501.7 jit_solution(18174793391187205027)
XLA Ops:
  12.6 14.0 %shard_map.111 = bf16[3,128,1024]{2,1,0:T(8,128)(2,1)S(1)} custom-call(bf16[128,4096]{1,0:T(8,128)(2,1)S(1)} %copy-done, bf16[3,4096,1024]{2,1,0:T(8,128)(2,1)} %bitcast.150, bf16[3,32,1,1024]{3,2,1,0:T(2,128)(2,1)S(1)} %broadcast_in_dim.120.m_ref), custom_call_target="tpu_custom_call" | custom-call | flops 3221225472 | bytes 29097984 | tf_op jit(solution)/shard_map/pallas_call | solution.py:66
  36.6 25.2 %collective-permute-done.1.a_ref = bf16[128,4096]{1,0:T(8,128)(2,1)S(1)} collective-permute-done((bf16[128,4096]{1,0:T(8,128)(2,1)S(1)}, bf16[128,4096]{1,0:T(8,128)(2,1)S(1)}, u32[]{:S(2)}, u32[]{:S(2)}) %collective-permute-start.1) | collective-permute-done | bytes 1048608 | tf_op jit(solution)/shard_map/ppermute | solution.py:132
  61.8 14.0 %shard_map.112 = bf16[3,128,1024]{2,1,0:T(8,128)(2,1)S(1)} custom-call(bf16[128,4096]{1,0:T(8,128)(2,1)S(1)} %collective-permute-done.a_ref, bf16[3,4096,1024]{2,1,0:T(8,128)(2,1)} %bitcast.151, bf16[3,32,1,1024]{3,2,1,0:T(2,128)(2,1)S(1)} %broadcast_in_dim.120.m_ref), custom_call_target="tpu_custom_call" | custom-call | flops 3221225472 | bytes 29097984 | tf_op jit(solution)/shard_map/pallas_call | solution.py:66
  75.9 14.0 %shard_map.113 = bf16[3,128,1024]{2,1,0:T(8,128)(2,1)S(1)} custom-call(bf16[128,4096]{1,0:T(8,128)(2,1)S(1)} %collective-permute-done.1.a_ref, bf16[3,4096,1024]{2,1,0:T(8,128)(2,1)} %bitcast.152, bf16[3,32,1,1024]{3,2,1,0:T(2,128)(2,1)S(1)} %broadcast_in_dim.120.m_ref), custom_call_target="tpu_custom_call" | custom-call | flops 3221225472 | bytes 29097984 | tf_op jit(solution)/shard_map/pallas_call | solution.py:66
  90.0 14.4 %shard_map.114 = bf16[3,128,1024]{2,1,0:T(8,128)(2,1)S(1)} custom-call(bf16[128,4096]{1,0:T(8,128)(2,1)S(1)} %collective-permute-done.2.a_ref, bf16[3,4096,1024]{2,1,0:T(8,128)(2,1)} %bitcast.153, bf16[3,32,1,1024]{3,2,1,0:T(2,128)(2,1)S(1)} %broadcast_in_dim.120.m_ref), custom_call_target="tpu_custom_call" | custom-call | flops 3221225472 | bytes 29097984 | tf_op jit(solution)/shard_map/pallas_call | solution.py:66
  124.5 6.6 %copy.126 = bf16[512,4096]{0,1:T(8,128)(2,1)} copy(bf16[512,4096]{1,0:T(8,128)(2,1)} %bitcast.156) | data formatting | bytes 8388608 | tf_op jit(solution)/shard_map/reshape | solution.py:288
  139.1 17.5 %collective-permute-done.3 = bf16[128,4096]{1,0:T(8,128)(2,1)} collective-permute-done((bf16[128,4096]{1,0:T(8,128)(2,1)}, bf16[128,4096]{1,0:T(8,128)(2,1)}, u32[]{:S(2)}, u32[]{:S(2)}) %collective-permute-start.3) | collective-permute-done | bytes 1048608 | tf_op jit(solution)/shard_map/ppermute | solution.py:171
  164.3 16.9 %collective-permute-done.4 = bf16[128,4096]{1,0:T(8,128)(2,1)} collective-permute-done((bf16[128,4096]{1,0:T(8,128)(2,1)}, bf16[128,4096]{1,0:T(8,128)(2,1)}, u32[]{:S(2)}, u32[]{:S(2)}) %collective-permute-start.4) | collective-permute-done | bytes 1048608 | tf_op jit(solution)/shard_map/ppermute | solution.py:171
  184.4 7.2 %shard_map.115 = bf16[1,512,4096]{2,1,0:T(8,128)(2,1)S(1)} custom-call(bf16[512,1024]{1,0:T(8,128)(2,1)S(1)} %copy.130.a_ref, bf16[1,1024,4096]{2,1,0:T(8,128)(2,1)} %bitcast.174, bf16[1,8,1,4096]{3,2,1,0:T(2,128)(2,1)S(1)} %copy-done.5), custom_call_target="tpu_custom_call" | custom-call | flops 4294967296 | bytes 16777216 | tf_op jit(solution)/shard_map/pallas_call | solution.py:66
  196.0 12.0 %collective-permute-done.5 = bf16[128,4096]{1,0:T(8,128)(2,1)S(1)} collective-permute-done((bf16[128,4096]{1,0:T(8,128)(2,1)}, bf16[128,4096]{1,0:T(8,128)(2,1)S(1)}, u32[]{:S(2)}, u32[]{:S(2)}) %collective-permute-start.5) | collective-permute-done | bytes 1048608 | tf_op jit(solution)/shard_map/ppermute | solution.py:171
  209.0 8.2 %shard_map.116 = f32[512,1024]{1,0:T(8,128)S(1)} custom-call(bf16[1,512,4096]{2,1,0:T(8,128)(2,1)} %bitcast.28.a_ref, bf16[1,1024,4096]{2,1,0:T(8,128)(2,1)} %bitcast.175, bf16[1,8,1,4096]{3,2,1,0:T(2,128)(2,1)S(1)} %copy-done.6), custom_call_target="tpu_custom_call" | custom-call | flops 4294967296 | bytes 14680064 | tf_op jit(solution)/shard_map/pallas_call | solution.py:95
  226.0 10.4 %convolution_convert_fusion.1 = bf16[4096,1024]{1,0:T(8,128)(2,1)} fusion(bf16[512,4096]{1,0:T(8,128)(2,1)} %bitcast.25, bf16[512,1024]{0,1:T(8,128)(2,1)} %bitcast.163), kind=kOutput, calls=%fused_computation.5 | convolution fusion | flops 4299161600 | bytes 13631488 | tf_op jit(solution)/shard_map/tm,tf->mf/dot_general | solution.py:326
  243.1 18.3 %collective-permute-done.6 = bf16[128,4096]{1,0:T(8,128)(2,1)} collective-permute-done((bf16[128,4096]{1,0:T(8,128)(2,1)}, bf16[128,4096]{1,0:T(8,128)(2,1)}, u32[]{:S(2)}, u32[]{:S(2)}) %collective-permute-start.6) | collective-permute-done | bytes 1048608 | tf_op jit(solution)/shard_map/ppermute | solution.py:205
  267.2 14.4 %while.23 = (s32[]{:T(128)}, f32[8,128,128]{2,1,0:T(8,128)}, s32[]{:T(128)}, bf16[8,8,128,128]{3,2,1,0:T(8,128)(2,1)}, s32[]{:T(128)}, /*index=5*/s32[]{:T(128)}, s32[]{:T(128)}, s32[]{:T(128)}) while((s32[]{:T(128)}, f32[8,128,128]{2,1,0:T(8,128)}, s32[]{:T(128)}, bf16[8,8,128,128]{3,2,1,0:T(8,128)(2,1)}, s32[]{:T(128)}, ...), condition=%wide.region_5.6_spmd, body=%wide.region_4.5_spmd.sunk | while | flops 262150 | bytes 1310863 | solution.py:244
  296.6 21.0 %convolution_convert_fusion = bf16[4096,3,1024]{2,0,1:T(8,128)(2,1)} fusion(bf16[512,4096]{0,1:T(8,128)(2,1)} %copy.126, bf16[1,512,1024]{2,1,0:T(8,128)(2,1)} %copy.137, bf16[1,512,1024]{2,1,0:T(8,128)(2,1)S(1)} %copy.136, bf16[1,512,1024]{2,1,0:T(8,128)(2,1)} %copy.133), kind=kOutput, calls=%fused_computation.2 | convolution fusion | flops 12906921984 | bytes 32505856 | tf_op jit(solution)/shard_map/tm,ptc->mpc/dot_general | solution.py:368
  320.5 19.4 %collective-permute-done.7 = bf16[128,4096]{1,0:T(8,128)(2,1)S(1)} collective-permute-done((bf16[128,4096]{1,0:T(8,128)(2,1)S(1)}, bf16[128,4096]{1,0:T(8,128)(2,1)S(1)}, u32[]{:S(2)}, u32[]{:S(2)}) %collective-permute-start.7) | collective-permute-done | bytes 1048608 | tf_op jit(solution)/shard_map/ppermute | solution.py:205
  339.9 24.9 %shard_map.117 = bf16[512,4096]{1,0:T(8,128)(2,1)} custom-call(bf16[3,512,1024]{2,1,0:T(8,128)(2,1)S(1)} %pad_maximum_fusion.a_ref, bf16[3,4096,1024]{2,1,0:T(8,128)(2,1)} %bitcast.154, bf16[3,32,1,1024]{3,2,1,0:T(2,128)(2,1)S(1)} %broadcast_in_dim.120.m_ref), custom_call_target="tpu_custom_call" | custom-call | flops 12884901888 | bytes 41943040 | tf_op jit(solution)/shard_map/pallas_call | solution.py:95
  366.3 21.1 %collective-permute-done.9 = bf16[128,4096]{1,0:T(8,128)(2,1)} collective-permute-done((bf16[128,4096]{1,0:T(8,128)(2,1)S(1)}, bf16[128,4096]{1,0:T(8,128)(2,1)}, u32[]{:S(2)}, u32[]{:S(2)}) %collective-permute-start.9) | collective-permute-done | bytes 1048608 | tf_op jit(solution)/shard_map/ppermute | solution.py:152
  392.3 25.3 %collective-permute-done.10 = bf16[128,4096]{1,0:T(8,128)(2,1)} collective-permute-done((bf16[128,4096]{1,0:T(8,128)(2,1)S(1)}, bf16[128,4096]{1,0:T(8,128)(2,1)}, u32[]{:S(2)}, u32[]{:S(2)}) %collective-permute-start.10) | collective-permute-done | bytes 1048608 | tf_op jit(solution)/shard_map/ppermute | solution.py:152
  424.1 7.2 %reshape.101 = f32[512,3,1024]{2,0,1:T(8,128)} reshape(f32[4,128,3,8,128]{4,3,1,0,2:T(8,128)} %broadcast_in_dim.118) | data formatting | bytes 12582912 | tf_op jit(solution)/shard_map/reshape | solution.py:376
  431.3 8.7 %collective-permute-done.8 = bf16[128,4096]{1,0:T(8,128)(2,1)S(1)} collective-permute-done((bf16[128,4096]{1,0:T(8,128)(2,1)}, bf16[128,4096]{1,0:T(8,128)(2,1)S(1)}, u32[]{:S(2)}, u32[]{:S(2)}) %collective-permute-start.8) | collective-permute-done | bytes 1048608 | tf_op jit(solution)/shard_map/ppermute | solution.py:205
  442.6 10.1 %collective-permute-done.11 = bf16[128,4096]{1,0:T(8,128)(2,1)} collective-permute-done((bf16[128,4096]{1,0:T(8,128)(2,1)}, bf16[128,4096]{1,0:T(8,128)(2,1)}, u32[]{:S(2)}, u32[]{:S(2)}) %collective-permute-start.11) | collective-permute-done | bytes 1048608 | tf_op jit(solution)/shard_map/ppermute | solution.py:152
  459.6 27.0 %reduce-scatter.3.cloned.1.call-done = bf16[512,3,1024]{2,0,1:T(8,128)(2,1)} async-done(((bf16[4096,3,1024]{2,0,1:T(8,128)(2,1)}), bf16[512,3,1024]{2,0,1:T(8,128)(2,1)}) %reduce-scatter.3.cloned.1.call-update) | async-done | bytes 3145744 | tf_op jit(solution)/shard_map/reduce_scatter | solution.py:369
  486.6 8.0 %multiply_multiply_fusion = f32[512,3,1024]{2,0,1:T(8,128)} fusion(f32[512,3,1024]{2,0,1:T(8,128)} %reshape.101, bf16[512,3,1024]{2,0,1:T(8,128)(2,1)} %reduce-scatter.3.cloned.1.call-done), kind=kLoop, calls=%fused_computation.6 | loop fusion | flops 4718592 | bytes 15728640 | tf_op jit(solution)/shard_map/mul | solution.py:377
  (190 shorter events, 134.9 us)
Async XLA Ops:
  7.2 151.8 %all-gather.5.cloned.1.call-start = ((), (), s32[]{:S(2)}) async-start(), calls=%async_computation.4 | async-start | bytes 2359296 | tf_op jit(solution)/shard_map/all_gather | solution.py:222
  7.2 28.5 %collective-permute-start = (bf16[128,4096]{1,0:T(8,128)(2,1)}, bf16[128,4096]{1,0:T(8,128)(2,1)S(1)}, u32[]{:S(2)}, u32[]{:S(2)}) collective-permute-start(bf16[128,4096]{1,0:T(8,128)(2,1)} %a_ref.1), channel_id=1, source_target_pairs={{0,1},{1,2},{2,3},{3,0},{4,5},{5,6},{6,7},{7,4},{8,9},{9,10},{10,1... | collective-permute-start | bytes 3145736 | tf_op jit(solution)/shard_map/ppermute | solution.py:132
  29.4 129.9 %copy-start.32 = (bf16[512,8]{0,1:T(8,128)(2,1)}, bf16[512,8]{0,1:T(8,128)(2,1)S(1)}, u32[]{:S(2)}) copy-start(bf16[512,8]{0,1:T(8,128)(2,1)S(1)} %get-tuple-element.142) | copy-start | bytes 24580
  35.7 26.1 %collective-permute-start.1 = (bf16[128,4096]{1,0:T(8,128)(2,1)S(1)}, bf16[128,4096]{1,0:T(8,128)(2,1)S(1)}, u32[]{:S(2)}, u32[]{:S(2)}) collective-permute-start(bf16[128,4096]{1,0:T(8,128)(2,1)S(1)} %collective-permute-done.a_ref), channel_id=1, source_target_pairs={{0,1},{1,2},{2,3},{3,0},{4,5},{5,6},{6,7},{7,4},{8,9},{9,10},{10,1... | collective-permute-start | bytes 3145736 | tf_op jit(solution)/shard_map/ppermute | solution.py:132
  36.6 25.3 %copy-start.18 = (bf16[4,128,4096]{2,1,0:T(8,128)(2,1)}, bf16[4,128,4096]{2,1,0:T(8,128)(2,1)S(1)}, u32[]{:S(2)}) copy-start(bf16[4,128,4096]{2,1,0:T(8,128)(2,1)S(1)} %bitcast_dynamic-update-slice_fusion.6) | copy-start | bytes 12582916
  36.6 39.3 %copy-start.20 = (bf16[3,4,128,1024]{3,2,1,0:T(8,128)(2,1)S(1)}, bf16[3,4,128,1024]{3,2,1,0:T(8,128)(2,1)}, u32[]{:S(2)}) copy-start(bf16[3,4,128,1024]{3,2,1,0:T(8,128)(2,1)} %copy-done.19) | copy-start | bytes 9437188
  61.8 28.2 %collective-permute-start.2 = (bf16[128,4096]{1,0:T(8,128)(2,1)S(1)}, bf16[128,4096]{1,0:T(8,128)(2,1)S(1)}, u32[]{:S(2)}, u32[]{:S(2)}) collective-permute-start(bf16[128,4096]{1,0:T(8,128)(2,1)S(1)} %collective-permute-done.1.a_ref), channel_id=1, source_target_pairs={{0,1},{1,2},{2,3},{3,0},{4,5},{5,6},{6,7},{7,4},{8,9},{9,10},{10,1... | collective-permute-start | bytes 3145736 | tf_op jit(solution)/shard_map/ppermute | solution.py:132
  118.1 148.2 %all-gather.7.cloned.1.call-start = ((), (), s32[]{:S(2)}) async-start(), calls=%async_computation.5 | async-start | bytes 2359296 | tf_op jit(solution)/shard_map/all_gather | solution.py:235
  123.3 35.9 %copy-start.15 = (bf16[512,8,128]{0,2,1:T(8,128)(2,1)}, bf16[512,8,128]{0,2,1:T(8,128)(2,1)S(1)}, u32[]{:S(2)}) copy-start(bf16[512,8,128]{0,2,1:T(8,128)(2,1)S(1)} %copy.87) | copy-start | bytes 3145732
  131.1 25.5 %collective-permute-start.3 = (bf16[128,4096]{1,0:T(8,128)(2,1)}, bf16[128,4096]{1,0:T(8,128)(2,1)}, u32[]{:S(2)}, u32[]{:S(2)}) collective-permute-start(bf16[128,4096]{1,0:T(8,128)(2,1)} %param.19), channel_id=1, source_target_pairs={{0,1},{1,2},{2,3},{3,0},{4,5},{5,6},{6,7},{7,4},{8,9},{9,10},{10,1... | collective-permute-start | bytes 3145736 | tf_op jit(solution)/shard_map/ppermute | solution.py:171
  156.6 24.6 %collective-permute-start.4 = (bf16[128,4096]{1,0:T(8,128)(2,1)}, bf16[128,4096]{1,0:T(8,128)(2,1)}, u32[]{:S(2)}, u32[]{:S(2)}) collective-permute-start(bf16[128,4096]{1,0:T(8,128)(2,1)} %collective-permute-done.3), channel_id=1, source_target_pairs={{0,1},{1,2},{2,3},{3,0},{4,5},{5,6},{6,7},{7,4},{8,9},{9,10},{10,1... | collective-permute-start | bytes 3145736 | tf_op jit(solution)/shard_map/ppermute | solution.py:171
  184.3 23.6 %collective-permute-start.5 = (bf16[128,4096]{1,0:T(8,128)(2,1)}, bf16[128,4096]{1,0:T(8,128)(2,1)S(1)}, u32[]{:S(2)}, u32[]{:S(2)}) collective-permute-start(bf16[128,4096]{1,0:T(8,128)(2,1)} %collective-permute-done.4), channel_id=1, source_target_pairs={{0,1},{1,2},{2,3},{3,0},{4,5},{5,6},{6,7},{7,4},{8,9},{9,10},{10,1... | collective-permute-start | bytes 3145736 | tf_op jit(solution)/shard_map/ppermute | solution.py:171
  225.7 230.0 %reduce-scatter.5.cloned.1.call-start = ((), (), s32[]{:S(2)}) async-start(), calls=%async_computation.3 | async-start | bytes 9437184 | tf_op jit(solution)/shard_map/reduce_scatter | solution.py:327
  236.3 250.3 %reduce-scatter.3.cloned.1.call-start = ((), (), s32[]{:S(2)}) async-start(), calls=%async_computation.2 | async-start | bytes 28311552 | tf_op jit(solution)/shard_map/reduce_scatter | solution.py:369
  238.7 22.8 %collective-permute-start.6 = (bf16[128,4096]{1,0:T(8,128)(2,1)}, bf16[128,4096]{1,0:T(8,128)(2,1)}, u32[]{:S(2)}, u32[]{:S(2)}) collective-permute-start(bf16[128,4096]{1,0:T(8,128)(2,1)} %dynamic-slice_bitcast_fusion.1), channel_id=1, source_target_pairs={{0,1},{1,2},{2,3},{3,0},{4,5},{5,6},{6,7},{7,4},{8,9},{9,10},{10,1... | collective-permute-start | bytes 3145736 | tf_op jit(solution)/shard_map/ppermute | solution.py:205
  319.6 20.3 %collective-permute-start.7 = (bf16[128,4096]{1,0:T(8,128)(2,1)S(1)}, bf16[128,4096]{1,0:T(8,128)(2,1)S(1)}, u32[]{:S(2)}, u32[]{:S(2)}) collective-permute-start(bf16[128,4096]{1,0:T(8,128)(2,1)S(1)} %fusion.10), channel_id=1, source_target_pairs={{0,1},{1,2},{2,3},{3,0},{4,5},{5,6},{6,7},{7,4},{8,9},{9,10},{10,1... | collective-permute-start | bytes 3145736 | tf_op jit(solution)/shard_map/ppermute | solution.py:205
  339.9 24.9 %copy-start.29 = (bf16[128,4096]{1,0:T(8,128)(2,1)}, bf16[128,4096]{1,0:T(8,128)(2,1)S(1)}, u32[]{:S(2)}) copy-start(bf16[128,4096]{1,0:T(8,128)(2,1)S(1)} %collective-permute-done.7) | copy-start | bytes 3145732
  364.8 24.8 %copy-start.40 = (s32[8,32]{1,0:T(8,128)S(1)}, s32[8,32]{1,0:T(8,128)}, u32[]{:S(2)}) copy-start(s32[8,32]{1,0:T(8,128)} %param.18) | copy-start | bytes 3076
  364.8 25.0 %copy-start.30 = (bf16[128,4096]{1,0:T(8,128)(2,1)S(1)}, bf16[128,4096]{1,0:T(8,128)(2,1)}, u32[]{:S(2)}) copy-start(bf16[128,4096]{1,0:T(8,128)(2,1)} %copy-done.29) | copy-start | bytes 3145732
  366.2 21.2 %collective-permute-start.9 = (bf16[128,4096]{1,0:T(8,128)(2,1)S(1)}, bf16[128,4096]{1,0:T(8,128)(2,1)}, u32[]{:S(2)}, u32[]{:S(2)}) collective-permute-start(bf16[128,4096]{1,0:T(8,128)(2,1)S(1)} %dynamic-slice_bitcast_fusion), channel_id=1, source_target_pairs={{0,1},{1,2},{2,3},{3,0},{4,5},{5,6},{6,7},{7,4},{8,9},{9,10},{10,1... | collective-permute-start | bytes 3145736 | tf_op jit(solution)/shard_map/ppermute | solution.py:152
  389.3 28.3 %collective-permute-start.10 = (bf16[128,4096]{1,0:T(8,128)(2,1)S(1)}, bf16[128,4096]{1,0:T(8,128)(2,1)}, u32[]{:S(2)}, u32[]{:S(2)}) collective-permute-start(bf16[128,4096]{1,0:T(8,128)(2,1)S(1)} %fusion.6), channel_id=1, source_target_pairs={{0,1},{1,2},{2,3},{3,0},{4,5},{5,6},{6,7},{7,4},{8,9},{9,10},{10,1... | collective-permute-start | bytes 3145736 | tf_op jit(solution)/shard_map/ppermute | solution.py:152
  389.8 30.9 %copy-start.36 = (s32[3,32,8]{1,2,0:T(8,128)S(1)}, s32[3,32,8]{1,2,0:T(8,128)}, u32[]{:S(2)}) copy-start(s32[3,32,8]{1,2,0:T(8,128)} %param.16) | copy-start | bytes 9220
  392.2 47.7 %collective-permute-start.8 = (bf16[128,4096]{1,0:T(8,128)(2,1)}, bf16[128,4096]{1,0:T(8,128)(2,1)S(1)}, u32[]{:S(2)}, u32[]{:S(2)}) collective-permute-start(bf16[128,4096]{1,0:T(8,128)(2,1)} %fusion.9), channel_id=1, source_target_pairs={{0,1},{1,2},{2,3},{3,0},{4,5},{5,6},{6,7},{7,4},{8,9},{9,10},{10,1... | collective-permute-start | bytes 3145736 | tf_op jit(solution)/shard_map/ppermute | solution.py:205
  420.7 32.0 %collective-permute-start.11 = (bf16[128,4096]{1,0:T(8,128)(2,1)}, bf16[128,4096]{1,0:T(8,128)(2,1)}, u32[]{:S(2)}, u32[]{:S(2)}) collective-permute-start(bf16[128,4096]{1,0:T(8,128)(2,1)} %fusion.5), channel_id=1, source_target_pairs={{0,1},{1,2},{2,3},{3,0},{4,5},{5,6},{6,7},{7,4},{8,9},{9,10},{10,1... | collective-permute-start | bytes 3145736 | tf_op jit(solution)/shard_map/ppermute | solution.py:152
  (33 other events, 228.9 us)
Sparse Core Ops, SparseCore 0:
  118.3 29.1 all-gather.4
  225.8 25.1 all-gather.6
  254.5 71.2 reduce-scatter.4
  329.7 156.8 reduce-scatter.2

commit v4 on v0

--- a/solution.py
+++ b/solution.py
@@ -374,7 +374,8 @@
         jnp.transpose(qkv_keep, (1, 0, 2)).astype(jnp.float32)[:, None, :, :, None],
         (slice_blocks, BLOCK, 3, col_blocks, BLOCK),
     ).reshape(slice_rows, 3, features)
-    qkv_grad = qkv_sum * qkv_keep * norm_factor
+    qkv_scale = lax.optimization_barrier(qkv_keep * norm_factor)
+    qkv_grad = qkv_sum * qkv_scale
     grad_proj = head_ring.advance(grad_proj)
     grad_proj_late = grad_proj
     token_sum = ring_scatter(

time: 498 us -> 498 us (level)
    mul x0 -> x2, local copies, waits for them, and re-layouts: none -> 7.35 us  [on_device(): qkv_scale = lax.optimization_barrier(qkv_keep * norm_factor)]
    reshape x1 -> x0, local copies, waits for them, and re-layouts: 7.26 us -> none  [on_device(): qkv_keep = jnp.broadcast_to(jnp.transpose(qkv_keep, (1, 0, 2)).astype(jnp...]
where the time goes in v4:
time: 498 us; the launch traced here: 488 us
  waiting for transfers between devices  220 us (44%)
  Pallas kernels  96 us (19%)
  matrix products  60.4 us (12%)
  local copies, waits for them, and re-layouts  49.9 us (10%)
  other arithmetic  42.6 us (9%)
  between operations  14.9 us (3%)
    pallas_call x5, Pallas kernels, masked_matmul_nn(): pl.pallas_call(_nn_kernel, grid=grid, in_specs=[pl.BlockSpec((m, tk), lam...  63.2 us
    ppermute x3, waiting for transfers between devices, ring_scatter(): arrived = lax.ppermute(running.astype(jnp.bfloat16), axis, step)  56.8 us
    ppermute x3, waiting for transfers between devices, advance(): lax.ppermute(self.running.astype(jnp.bfloat16), self.axis, self.step)  49.5 us
    ppermute x3, waiting for transfers between devices, advance(): moved = lax.ppermute(self.moving, self.axis, self.step)  47.6 us
    reduce_scatter x1, waiting for transfers between devices, on_device(): lax.psum_scatter(qkv_part.astype(jnp.bfloat16), 'ctx', scatter_dimension=...  36.5 us
    pallas_call x2, Pallas kernels, masked_matmul_nt(): pl.pallas_call(_nt_kernel, grid=grid, in_specs=[pl.BlockSpec((None, m, tk...  32.8 us
    ppermute x3, waiting for transfers between devices, ring_gather(): moving = lax.ppermute(moving, axis, step)  29.2 us
    dot_general x1, matrix products, on_device(): jnp.einsum('tm,ptc->mpc', gathered, grad_proj, preferred_element_type=jnp...  20.9 us
  transfers between devices with their start and end apart: 16, of which 12 were waited for; matrix products, arithmetic and copies ran while one was open for 25% of the time, Pallas kernels for 15%

profile of v4, /device:TPU:0, one launch (start us, length us, event | category | flops | bytes accessed | tf_op | source)
XLA Modules:
  0.0 487.9 jit_solution(16940013160359001178)
XLA Ops:
  16.7 14.0 %shard_map.111 = bf16[3,128,1024]{2,1,0:T(8,128)(2,1)S(1)} custom-call(bf16[128,4096]{1,0:T(8,128)(2,1)S(1)} %copy-done, bf16[3,4096,1024]{2,1,0:T(8,128)(2,1)} %bitcast.140, bf16[3,32,1,1024]{3,2,1,0:T(2,128)(2,1)S(1)} %broadcast_in_dim.120.m_ref), custom_call_target="tpu_custom_call" | custom-call | flops 3221225472 | bytes 29097984 | tf_op jit(solution)/shard_map/pallas_call | solution.py:66
  37.1 24.7 %collective-permute-done.1.a_ref = bf16[128,4096]{1,0:T(8,128)(2,1)S(1)} collective-permute-done((bf16[128,4096]{1,0:T(8,128)(2,1)S(1)}, bf16[128,4096]{1,0:T(8,128)(2,1)S(1)}, u32[]{:S(2)}, u32[]{:S(2)}) %collective-permute-start.1) | collective-permute-done | bytes 1048608 | tf_op jit(solution)/shard_map/ppermute | solution.py:132
  61.8 14.0 %shard_map.112 = bf16[3,128,1024]{2,1,0:T(8,128)(2,1)S(1)} custom-call(bf16[128,4096]{1,0:T(8,128)(2,1)S(1)} %collective-permute-done.a_ref, bf16[3,4096,1024]{2,1,0:T(8,128)(2,1)} %bitcast.141, bf16[3,32,1,1024]{3,2,1,0:T(2,128)(2,1)S(1)} %broadcast_in_dim.120.m_ref), custom_call_target="tpu_custom_call" | custom-call | flops 3221225472 | bytes 29097984 | tf_op jit(solution)/shard_map/pallas_call | solution.py:66
  75.9 14.0 %shard_map.113 = bf16[3,128,1024]{2,1,0:T(8,128)(2,1)S(1)} custom-call(bf16[128,4096]{1,0:T(8,128)(2,1)S(1)} %collective-permute-done.1.a_ref, bf16[3,4096,1024]{2,1,0:T(8,128)(2,1)} %bitcast.142, bf16[3,32,1,1024]{3,2,1,0:T(2,128)(2,1)S(1)} %broadcast_in_dim.120.m_ref), custom_call_target="tpu_custom_call" | custom-call | flops 3221225472 | bytes 29097984 | tf_op jit(solution)/shard_map/pallas_call | solution.py:66
  90.0 14.0 %shard_map.114 = bf16[3,128,1024]{2,1,0:T(8,128)(2,1)S(1)} custom-call(bf16[128,4096]{1,0:T(8,128)(2,1)S(1)} %collective-permute-done.2.a_ref, bf16[3,4096,1024]{2,1,0:T(8,128)(2,1)} %bitcast.143, bf16[3,32,1,1024]{3,2,1,0:T(2,128)(2,1)S(1)} %broadcast_in_dim.120.m_ref), custom_call_target="tpu_custom_call" | custom-call | flops 3221225472 | bytes 29097984 | tf_op jit(solution)/shard_map/pallas_call | solution.py:66
  116.9 4.6 select_convert_fusion.1
  125.1 17.3 %collective-permute-done.3 = bf16[128,4096]{1,0:T(8,128)(2,1)} collective-permute-done((bf16[128,4096]{1,0:T(8,128)(2,1)}, bf16[128,4096]{1,0:T(8,128)(2,1)}, u32[]{:S(2)}, u32[]{:S(2)}) %collective-permute-start.3) | collective-permute-done | bytes 1048608 | tf_op jit(solution)/shard_map/ppermute | solution.py:171
  149.9 17.1 %collective-permute-done.4 = bf16[128,4096]{1,0:T(8,128)(2,1)} collective-permute-done((bf16[128,4096]{1,0:T(8,128)(2,1)}, bf16[128,4096]{1,0:T(8,128)(2,1)}, u32[]{:S(2)}, u32[]{:S(2)}) %collective-permute-start.4) | collective-permute-done | bytes 1048608 | tf_op jit(solution)/shard_map/ppermute | solution.py:171
  170.3 7.3 %shard_map.115 = bf16[1,512,4096]{2,1,0:T(8,128)(2,1)S(1)} custom-call(bf16[512,1024]{1,0:T(8,128)(2,1)S(1)} %copy.122.a_ref, bf16[1,1024,4096]{2,1,0:T(8,128)(2,1)} %bitcast.172, bf16[1,8,1,4096]{3,2,1,0:T(2,128)(2,1)S(1)} %copy-done.3), custom_call_target="tpu_custom_call" | custom-call | flops 4294967296 | bytes 16777216 | tf_op jit(solution)/shard_map/pallas_call | solution.py:66
  180.7 13.2 %collective-permute-done.5 = bf16[128,4096]{1,0:T(8,128)(2,1)S(1)} collective-permute-done((bf16[128,4096]{1,0:T(8,128)(2,1)}, bf16[128,4096]{1,0:T(8,128)(2,1)S(1)}, u32[]{:S(2)}, u32[]{:S(2)}) %collective-permute-start.5) | collective-permute-done | bytes 1048608 | tf_op jit(solution)/shard_map/ppermute | solution.py:171
  195.4 8.2 %shard_map.116 = f32[512,1024]{1,0:T(8,128)S(1)} custom-call(bf16[1,512,4096]{2,1,0:T(8,128)(2,1)} %bitcast.27.a_ref, bf16[1,1024,4096]{2,1,0:T(8,128)(2,1)} %bitcast.173, bf16[1,8,1,4096]{3,2,1,0:T(2,128)(2,1)S(1)} %copy-done.3), custom_call_target="tpu_custom_call" | custom-call | flops 4294967296 | bytes 14680064 | tf_op jit(solution)/shard_map/pallas_call | solution.py:95
  212.1 9.2 %convolution_convert_fusion.1 = bf16[4096,1024]{1,0:T(8,128)(2,1)} fusion(bf16[512,4096]{1,0:T(8,128)(2,1)} %bitcast.24, bf16[512,1024]{0,1:T(8,128)(2,1)S(1)} %bitcast.165), kind=kOutput, calls=%fused_computation.5 | convolution fusion | flops 4299161600 | bytes 13631488 | tf_op jit(solution)/shard_map/tm,tf->mf/dot_general | solution.py:326
  227.0 19.5 %collective-permute-done.6 = bf16[128,4096]{1,0:T(8,128)(2,1)} collective-permute-done((bf16[128,4096]{1,0:T(8,128)(2,1)}, bf16[128,4096]{1,0:T(8,128)(2,1)}, u32[]{:S(2)}, u32[]{:S(2)}) %collective-permute-start.6) | collective-permute-done | bytes 1048608 | tf_op jit(solution)/shard_map/ppermute | solution.py:205
  249.5 8.1 %while.23 = (s32[]{:T(128)}, f32[8,128,128]{2,1,0:T(8,128)S(1)}, s32[]{:T(128)}, bf16[8,8,128,128]{3,2,1,0:T(8,128)(2,1)}, s32[]{:T(128)}, /*index=5*/s32[]{:T(128)}, s32[]{:T(128)}, s32[]{:T(128)}) while((s32[]{:T(128)}, f32[8,128,128]{2,1,0:T(8,128)S(1)}, s32[]{:T(128)}, bf16[8,8,128,128]{3,2,1,0:T(8,128)(2,1)}, s32[]{:T(128)}, ...), condition=%wide.region_5.6_spmd, body=%wide.region_4.5_spmd.sunk | while | flops 262150 | bytes 1310863 | solution.py:244
  272.3 20.9 %convolution_convert_fusion = bf16[4096,3,1024]{2,0,1:T(8,128)(2,1)} fusion(bf16[512,4096,1]{1,0,2:T(8,128)(2,1)} %bitcast.169, bf16[1,512,1024]{2,1,0:T(8,128)(2,1)} %copy.125, bf16[1,512,1024]{2,1,0:T(8,128)(2,1)S(1)} %copy.124, bf16[1,512,1024]{2,1,0:T(8,128)(2,1)S(1)} %copy-done.21), kind=kOutput, calls=%fused_computation.2 | convolution fusion | flops 12906921984 | bytes 32505856 | tf_op jit(solution)/shard_map/tm,ptc->mpc/dot_general | solution.py:368
  295.9 21.0 %collective-permute-done.7 = bf16[128,4096]{1,0:T(8,128)(2,1)S(1)} collective-permute-done((bf16[128,4096]{1,0:T(8,128)(2,1)S(1)}, bf16[128,4096]{1,0:T(8,128)(2,1)S(1)}, u32[]{:S(2)}, u32[]{:S(2)}) %collective-permute-start.7) | collective-permute-done | bytes 1048608 | tf_op jit(solution)/shard_map/ppermute | solution.py:205
  316.9 24.6 %shard_map.117 = bf16[512,4096]{1,0:T(8,128)(2,1)} custom-call(bf16[3,512,1024]{2,1,0:T(8,128)(2,1)S(1)} %pad_maximum_fusion.a_ref, bf16[3,4096,1024]{2,1,0:T(8,128)(2,1)} %bitcast.144, bf16[3,32,1,1024]{3,2,1,0:T(2,128)(2,1)S(1)} %broadcast_in_dim.120.m_ref), custom_call_target="tpu_custom_call" | custom-call | flops 12884901888 | bytes 41943040 | tf_op jit(solution)/shard_map/pallas_call | solution.py:95
  343.2 21.8 %collective-permute-done.9 = bf16[128,4096]{1,0:T(8,128)(2,1)S(1)} collective-permute-done((bf16[128,4096]{1,0:T(8,128)(2,1)S(1)}, bf16[128,4096]{1,0:T(8,128)(2,1)S(1)}, u32[]{:S(2)}, u32[]{:S(2)}) %collective-permute-start.9) | collective-permute-done | bytes 1048608 | tf_op jit(solution)/shard_map/ppermute | solution.py:152
  369.2 25.2 %collective-permute-done.10 = bf16[128,4096]{1,0:T(8,128)(2,1)} collective-permute-done((bf16[128,4096]{1,0:T(8,128)(2,1)S(1)}, bf16[128,4096]{1,0:T(8,128)(2,1)}, u32[]{:S(2)}, u32[]{:S(2)}) %collective-permute-start.10) | collective-permute-done | bytes 1048608 | tf_op jit(solution)/shard_map/ppermute | solution.py:152
  400.6 7.3 %mul.108 = f32[512,3,1024]{2,0,1:T(8,128)} reshape(f32[4,128,3,8,128]{4,3,1,0,2:T(8,128)} %broadcast_in_dim.118) | data formatting | bytes 12582912 | tf_op jit(solution)/shard_map/mul | solution.py:377
  407.8 9.0 %collective-permute-done.8 = bf16[128,4096]{1,0:T(8,128)(2,1)S(1)} collective-permute-done((bf16[128,4096]{1,0:T(8,128)(2,1)}, bf16[128,4096]{1,0:T(8,128)(2,1)S(1)}, u32[]{:S(2)}, u32[]{:S(2)}) %collective-permute-start.8) | collective-permute-done | bytes 1048608 | tf_op jit(solution)/shard_map/ppermute | solution.py:205
  419.6 9.8 %collective-permute-done.11 = bf16[128,4096]{1,0:T(8,128)(2,1)} collective-permute-done((bf16[128,4096]{1,0:T(8,128)(2,1)}, bf16[128,4096]{1,0:T(8,128)(2,1)}, u32[]{:S(2)}, u32[]{:S(2)}) %collective-permute-start.11) | collective-permute-done | bytes 1048608 | tf_op jit(solution)/shard_map/ppermute | solution.py:152
  436.4 36.5 %reduce-scatter.3.cloned.1.call-done = bf16[512,3,1024]{2,0,1:T(8,128)(2,1)} async-done(((bf16[4096,3,1024]{2,0,1:T(8,128)(2,1)}), bf16[512,3,1024]{2,0,1:T(8,128)(2,1)}) %reduce-scatter.3.cloned.1.call-update) | async-done | bytes 3145744 | tf_op jit(solution)/shard_map/reduce_scatter | solution.py:369
  472.9 8.1 %convert_multiply_fusion = f32[512,3,1024]{2,0,1:T(8,128)} fusion(f32[512,3,1024]{2,0,1:T(8,128)} %mul.108, bf16[512,3,1024]{2,0,1:T(8,128)(2,1)} %reduce-scatter.3.cloned.1.call-done), kind=kLoop, calls=%fused_computation.6 | loop fusion | flops 3145728 | bytes 15728640 | tf_op jit(solution)/shard_map/mul | solution.py:378
  (174 shorter events, 111.5 us)
Async XLA Ops:
  7.2 137.6 %all-gather.5.cloned.1.call-start = ((), (), s32[]{:S(2)}) async-start(), calls=%async_computation.4 | async-start | bytes 2359296 | tf_op jit(solution)/shard_map/all_gather | solution.py:222
  7.2 28.5 %collective-permute-start = (bf16[128,4096]{1,0:T(8,128)(2,1)}, bf16[128,4096]{1,0:T(8,128)(2,1)S(1)}, u32[]{:S(2)}, u32[]{:S(2)}) collective-permute-start(bf16[128,4096]{1,0:T(8,128)(2,1)} %a_ref.1), channel_id=1, source_target_pairs={{0,1},{1,2},{2,3},{3,0},{4,5},{5,6},{6,7},{7,4},{8,9},{9,10},{10,1... | collective-permute-start | bytes 3145736 | tf_op jit(solution)/shard_map/ppermute | solution.py:132
  14.2 130.6 %copy-start.28 = (bf16[512,8]{0,1:T(8,128)(2,1)}, bf16[512,8]{0,1:T(8,128)(2,1)S(1)}, u32[]{:S(2)}) copy-start(bf16[512,8]{0,1:T(8,128)(2,1)S(1)} %get-tuple-element.142) | copy-start | bytes 24580
  15.5 101.3 %copy-start.31 = (bf16[512,8]{0,1:T(8,128)(2,1)}, bf16[512,8]{0,1:T(8,128)(2,1)S(1)}, u32[]{:S(2)}) copy-start(bf16[512,8]{0,1:T(8,128)(2,1)S(1)} %get-tuple-element.144) | copy-start | bytes 24580
  35.7 26.1 %collective-permute-start.1 = (bf16[128,4096]{1,0:T(8,128)(2,1)S(1)}, bf16[128,4096]{1,0:T(8,128)(2,1)S(1)}, u32[]{:S(2)}, u32[]{:S(2)}) collective-permute-start(bf16[128,4096]{1,0:T(8,128)(2,1)S(1)} %collective-permute-done.a_ref), channel_id=1, source_target_pairs={{0,1},{1,2},{2,3},{3,0},{4,5},{5,6},{6,7},{7,4},{8,9},{9,10},{10,1... | collective-permute-start | bytes 3145736 | tf_op jit(solution)/shard_map/ppermute | solution.py:132
  37.1 38.7 %copy-start.20 = (bf16[4,128,4096]{2,1,0:T(8,128)(2,1)}, bf16[4,128,4096]{2,1,0:T(8,128)(2,1)S(1)}, u32[]{:S(2)}) copy-start(bf16[4,128,4096]{2,1,0:T(8,128)(2,1)S(1)} %bitcast_dynamic-update-slice_fusion.3) | copy-start | bytes 12582916
  61.8 28.2 %collective-permute-start.2 = (bf16[128,4096]{1,0:T(8,128)(2,1)S(1)}, bf16[128,4096]{1,0:T(8,128)(2,1)S(1)}, u32[]{:S(2)}, u32[]{:S(2)}) collective-permute-start(bf16[128,4096]{1,0:T(8,128)(2,1)S(1)} %collective-permute-done.1.a_ref), channel_id=1, source_target_pairs={{0,1},{1,2},{2,3},{3,0},{4,5},{5,6},{6,7},{7,4},{8,9},{9,10},{10,1... | collective-permute-start | bytes 3145736 | tf_op jit(solution)/shard_map/ppermute | solution.py:132
  113.1 136.3 %all-gather.7.cloned.1.call-start = ((), (), s32[]{:S(2)}) async-start(), calls=%async_computation.5 | async-start | bytes 2359296 | tf_op jit(solution)/shard_map/all_gather | solution.py:235
  116.8 28.1 %copy-start.10 = (bf16[1,512,1024]{1,2,0:T(8,128)(2,1)}, bf16[1,512,1024]{1,2,0:T(8,128)(2,1)S(1)}, u32[]{:S(2)}) copy-start(bf16[1,512,1024]{1,2,0:T(8,128)(2,1)S(1)} %copy.121) | copy-start | bytes 3145732
  116.8 25.6 %collective-permute-start.3 = (bf16[128,4096]{1,0:T(8,128)(2,1)}, bf16[128,4096]{1,0:T(8,128)(2,1)}, u32[]{:S(2)}, u32[]{:S(2)}) collective-permute-start(bf16[128,4096]{1,0:T(8,128)(2,1)} %param.19), channel_id=1, source_target_pairs={{0,1},{1,2},{2,3},{3,0},{4,5},{5,6},{6,7},{7,4},{8,9},{9,10},{10,1... | collective-permute-start | bytes 3145736 | tf_op jit(solution)/shard_map/ppermute | solution.py:171
  142.4 24.6 %collective-permute-start.4 = (bf16[128,4096]{1,0:T(8,128)(2,1)}, bf16[128,4096]{1,0:T(8,128)(2,1)}, u32[]{:S(2)}, u32[]{:S(2)}) collective-permute-start(bf16[128,4096]{1,0:T(8,128)(2,1)} %collective-permute-done.3), channel_id=1, source_target_pairs={{0,1},{1,2},{2,3},{3,0},{4,5},{5,6},{6,7},{7,4},{8,9},{9,10},{10,1... | collective-permute-start | bytes 3145736 | tf_op jit(solution)/shard_map/ppermute | solution.py:171
  170.1 23.8 %collective-permute-start.5 = (bf16[128,4096]{1,0:T(8,128)(2,1)}, bf16[128,4096]{1,0:T(8,128)(2,1)S(1)}, u32[]{:S(2)}, u32[]{:S(2)}) collective-permute-start(bf16[128,4096]{1,0:T(8,128)(2,1)} %collective-permute-done.4), channel_id=1, source_target_pairs={{0,1},{1,2},{2,3},{3,0},{4,5},{5,6},{6,7},{7,4},{8,9},{9,10},{10,1... | collective-permute-start | bytes 3145736 | tf_op jit(solution)/shard_map/ppermute | solution.py:171
  212.1 220.4 %reduce-scatter.5.cloned.1.call-start = ((), (), s32[]{:S(2)}) async-start(), calls=%async_computation.3 | async-start | bytes 9437184 | tf_op jit(solution)/shard_map/reduce_scatter | solution.py:327
  221.3 251.6 %reduce-scatter.3.cloned.1.call-start = ((), (), s32[]{:S(2)}) async-start(), calls=%async_computation.2 | async-start | bytes 28311552 | tf_op jit(solution)/shard_map/reduce_scatter | solution.py:369
  223.7 22.9 %collective-permute-start.6 = (bf16[128,4096]{1,0:T(8,128)(2,1)}, bf16[128,4096]{1,0:T(8,128)(2,1)}, u32[]{:S(2)}, u32[]{:S(2)}) collective-permute-start(bf16[128,4096]{1,0:T(8,128)(2,1)} %dynamic-slice_bitcast_fusion.1), channel_id=1, source_target_pairs={{0,1},{1,2},{2,3},{3,0},{4,5},{5,6},{6,7},{7,4},{8,9},{9,10},{10,1... | collective-permute-start | bytes 3145736 | tf_op jit(solution)/shard_map/ppermute | solution.py:205
  295.2 21.7 %collective-permute-start.7 = (bf16[128,4096]{1,0:T(8,128)(2,1)S(1)}, bf16[128,4096]{1,0:T(8,128)(2,1)S(1)}, u32[]{:S(2)}, u32[]{:S(2)}) collective-permute-start(bf16[128,4096]{1,0:T(8,128)(2,1)S(1)} %fusion.9), channel_id=1, source_target_pairs={{0,1},{1,2},{2,3},{3,0},{4,5},{5,6},{6,7},{7,4},{8,9},{9,10},{10,1... | collective-permute-start | bytes 3145736 | tf_op jit(solution)/shard_map/ppermute | solution.py:205
  316.9 24.6 %copy-start.25 = (bf16[128,4096]{1,0:T(8,128)(2,1)}, bf16[128,4096]{1,0:T(8,128)(2,1)S(1)}, u32[]{:S(2)}) copy-start(bf16[128,4096]{1,0:T(8,128)(2,1)S(1)} %collective-permute-done.7) | copy-start | bytes 3145732
  341.4 25.1 %copy-start.35 = (s32[8,32]{1,0:T(8,128)S(1)}, s32[8,32]{1,0:T(8,128)}, u32[]{:S(2)}) copy-start(s32[8,32]{1,0:T(8,128)} %param.18) | copy-start | bytes 3076
  341.4 25.2 %copy-start.26 = (bf16[128,4096]{1,0:T(8,128)(2,1)S(1)}, bf16[128,4096]{1,0:T(8,128)(2,1)}, u32[]{:S(2)}) copy-start(bf16[128,4096]{1,0:T(8,128)(2,1)} %copy-done.25) | copy-start | bytes 3145732
  343.1 21.8 %collective-permute-start.9 = (bf16[128,4096]{1,0:T(8,128)(2,1)S(1)}, bf16[128,4096]{1,0:T(8,128)(2,1)S(1)}, u32[]{:S(2)}, u32[]{:S(2)}) collective-permute-start(bf16[128,4096]{1,0:T(8,128)(2,1)S(1)} %dynamic-slice_bitcast_fusion), channel_id=1, source_target_pairs={{0,1},{1,2},{2,3},{3,0},{4,5},{5,6},{6,7},{7,4},{8,9},{9,10},{10,1... | collective-permute-start | bytes 3145736 | tf_op jit(solution)/shard_map/ppermute | solution.py:152
  366.4 28.1 %collective-permute-start.10 = (bf16[128,4096]{1,0:T(8,128)(2,1)S(1)}, bf16[128,4096]{1,0:T(8,128)(2,1)}, u32[]{:S(2)}, u32[]{:S(2)}) collective-permute-start(bf16[128,4096]{1,0:T(8,128)(2,1)S(1)} %fusion.5), channel_id=1, source_target_pairs={{0,1},{1,2},{2,3},{3,0},{4,5},{5,6},{6,7},{7,4},{8,9},{9,10},{10,1... | collective-permute-start | bytes 3145736 | tf_op jit(solution)/shard_map/ppermute | solution.py:152
  366.6 30.6 %copy-start.34 = (s32[3,32,8]{1,2,0:T(8,128)S(1)}, s32[3,32,8]{1,2,0:T(8,128)}, u32[]{:S(2)}) copy-start(s32[3,32,8]{1,2,0:T(8,128)} %param.16) | copy-start | bytes 9220
  369.2 47.6 %collective-permute-start.8 = (bf16[128,4096]{1,0:T(8,128)(2,1)}, bf16[128,4096]{1,0:T(8,128)(2,1)S(1)}, u32[]{:S(2)}, u32[]{:S(2)}) collective-permute-start(bf16[128,4096]{1,0:T(8,128)(2,1)} %fusion.8), channel_id=1, source_target_pairs={{0,1},{1,2},{2,3},{3,0},{4,5},{5,6},{6,7},{7,4},{8,9},{9,10},{10,1... | collective-permute-start | bytes 3145736 | tf_op jit(solution)/shard_map/ppermute | solution.py:205
  397.2 32.2 %collective-permute-start.11 = (bf16[128,4096]{1,0:T(8,128)(2,1)}, bf16[128,4096]{1,0:T(8,128)(2,1)}, u32[]{:S(2)}, u32[]{:S(2)}) collective-permute-start(bf16[128,4096]{1,0:T(8,128)(2,1)} %fusion.4), channel_id=1, source_target_pairs={{0,1},{1,2},{2,3},{3,0},{4,5},{5,6},{6,7},{7,4},{8,9},{9,10},{10,1... | collective-permute-start | bytes 3145736 | tf_op jit(solution)/shard_map/ppermute | solution.py:152
  (28 other events, 232.3 us)
Sparse Core Ops, SparseCore 0:
  113.2 29.1 all-gather.4
  212.2 25.0 all-gather.6
  240.7 71.2 reduce-scatter.4
  316.0 156.8 reduce-scatter.2
